TPU v7x, 128 devices: a whole 4x4x4 slice. The times are simulated.
128 devices in a mesh: region: 8 (over y, core), node: 16 (over x, z).
Axes of the slice: x: 4, y: 4, z: 4, core: 2. Of those that a mesh axis runs over, the one named last changes fastest.
Arguments:
- impedance: float32 [16, 4096, 4096], P('region', 'node'), as said below
- source_amp: float32 [16, 64, 4096], P('region', None, 'node'), may hold values from -6 to 6
- source_angle: float32 [16, 4096], P('region', 'node'), may hold values from -3.140625 to 3.140625
- impulse_taps: float32 [512, 131072], P(None, ('region', 'node'))
- incident: float32 [515, 131072], P(None, ('region', 'node')), may hold values from -6 to 6
- conductance: float32 [131072], P(('region', 'node')), may hold values from 0.5 to 2
- attach: int32 [131072], P(('region', 'node')), may hold values from 0 to 511
- pair_slot: int32 [128, 1024], P(('region', 'node')), may hold values from 0 to 1024, as said below
- fault_node: int32 [16, 64], P('region'), may hold values from 0 to 4095
- fault_step: int32 [16, 64], P('region'), may hold values from 0 to 7
- fault_res: float32 [16, 64], P('region'), may hold values from 0.1 to 1
Outputs:
- voltages: float32 [8, 16, 64, 4096], P(None, 'region', None, 'node')
Inputs may be any that keep to these rules, and one draw needn't show every extreme that they name: impedance[s] is a symmetric matrix for every s. `pair_slot`: row d (d = region index * 16 + node index) holds at position e * 8 + s, for each device e and slot s, a line end of device d paired with the one named at position d * 8 + s of row e, or 1024 where that slot is empty; a slot is filled in row d exactly when its mirror in row e is filled; each line end stands in at most one slot; in every draw some device pair fills all 8 slots.
All inputs are finite; a program needn't handle non-finite values.
Results may differ from a plain program's by a relative error of at most 0.0001.
Values sent between devices are 32-bit elements; how exact they have to be, the bound alone decides.
No kernel may reach another device: no remote copies, remote signals or barrier semaphores. Data moves between devices by JAX's collectives and lax.ppermute only.
A program may use at most 128 MiB of HBM per device.

v0:
```python
import math

import jax
import jax.numpy as jnp
from jax import lax
from jax.sharding import PartitionSpec as P

WINDOW_STEPS = 4
WINDOW_COUNT = 2


omega_step = 2.0 * math.pi / 400.0
PRECISE = lax.Precision.HIGHEST


def mm(spec, a, b):
    return jnp.einsum(spec, a, b, precision=PRECISE, preferred_element_type=jnp.float32)


def body(
    impedance,
    source_amp,
    source_angle,
    impulse_taps,
    incident,
    conductance,
    attach,
    pair_slot,
    fault_node,
    fault_step,
    fault_res,
):
    subnets, rows, order = impedance.shape
    cases = source_amp.shape[1]
    tap_len, ends = impulse_taps.shape
    past = incident.shape[0]
    steps = WINDOW_STEPS
    total = WINDOW_STEPS * WINDOW_COUNT
    n_node = order // rows
    row_ids = lax.axis_index("node") * rows + lax.iota(jnp.int32, rows)

    attach_map = (attach[:, None] == lax.iota(jnp.int32, subnets * rows)[None, :]).astype(jnp.float32)

    onehot = (fault_node[:, :, None] == lax.iota(jnp.int32, order)[None, None, :]).astype(jnp.float32)
    fault_colT = mm("srj,scj->scr", impedance, onehot)
    owner = (fault_node[:, :, None] == row_ids[None, None, :]).astype(jnp.float32)
    self_part = jnp.sum(fault_colT * owner, axis=2)

    flip = (lax.iota(jnp.int32, tap_len)[:, None] + lax.iota(jnp.int32, tap_len)[None, :] == tap_len - 1).astype(
        jnp.float32
    )
    taps_rev = mm("uj,jk->uk", flip, impulse_taps)
    padded = jnp.concatenate([incident, jnp.zeros((tap_len + total - 1 - past, ends), jnp.float32)], axis=0)
    base = jnp.stack([jnp.sum(taps_rev * padded[t : t + tap_len], axis=0) for t in range(total)])
    base_node = mm("tk,kr->tr", base, attach_map).reshape(total, subnets, rows)

    amp_cos = source_amp * jnp.cos(source_angle)[:, None, :]
    amp_sin = source_amp * jnp.sin(source_angle)[:, None, :]
    sources = lax.all_gather(jnp.concatenate([amp_cos, amp_sin], axis=1), "node", axis=2, tiled=True)
    h0 = jnp.transpose(base_node[:steps], (1, 0, 2))
    part_cos = jnp.sum(fault_colT * amp_cos, axis=2)
    part_sin = jnp.sum(fault_colT * amp_sin, axis=2)
    part_h = mm("sci,sti->stc", fault_colT, h0)
    partials = jnp.concatenate(
        [part_cos[:, None], part_sin[:, None], part_h, self_part[:, None]], axis=1
    ).reshape(subnets, -1)
    pad_len = 2 * rows - partials.shape[1]
    partials = jnp.concatenate([partials, jnp.zeros((subnets, pad_len), jnp.float32)], axis=1)
    small = jnp.concatenate([h0, partials.reshape(subnets, 2, rows)], axis=1)
    small = jnp.broadcast_to(small[None], (n_node,) + small.shape)
    small = lax.all_to_all(small, "node", 0, 0, tiled=True)
    h0_full = jnp.transpose(small[:, :, :steps], (1, 2, 0, 3)).reshape(subnets, steps, order)
    prod = mm("srj,scj->scr", impedance, jnp.concatenate([sources, h0_full], axis=1))
    sums = jnp.sum(small[:, :, steps:], axis=0).reshape(subnets, 2 * rows)
    sums = sums[:, : 7 * cases].reshape(subnets, 7, cases)
    fault_self = sums[:, 6]
    denominator = fault_self + fault_res

    results = []
    waves = []
    for t in range(steps):
        cw = math.cos(omega_step * t)
        sw = math.sin(omega_step * t)
        open_v = cw * prod[:, :cases] - sw * prod[:, cases : 2 * cases] + prod[:, 2 * cases + t][:, None, :]
        at_fault = cw * sums[:, 0] - sw * sums[:, 1] + sums[:, 2 + t]
        current = jnp.where(fault_step <= t, at_fault / denominator, 0.0)
        voltage = open_v - current[:, :, None] * fault_colT
        results.append(voltage)
        at_ends = mm("sci,ksi->ck", voltage, attach_map.reshape(ends, subnets, rows))
        waves.append(2.0 * conductance[None, :] * at_ends - base[t][None, :])

    slot_row = pair_slot[0]
    end_ids = lax.iota(jnp.int32, ends)
    selector = (end_ids[:, None] == slot_row[None, :]).astype(jnp.float32)
    wave_block = jnp.stack(waves).reshape(steps * cases, ends)
    outgoing = mm("kp,mk->pm", selector, wave_block)
    incoming = lax.all_to_all(outgoing, ("region", "node"), 0, 0, tiled=True)
    far = mm("pm,kp->mk", incoming, selector).reshape(steps, cases, ends)

    inj_list = []
    for t in range(steps, total):
        history = base[t][None, :]
        for j in range(t - steps + 1):
            history = history + impulse_taps[j][None, :] * far[t - steps - j]
        node_hist = mm("ck,ksi->sci", history, attach_map.reshape(ends, subnets, rows))
        phase = jnp.cos(omega_step * t + source_angle)
        inj_list.append(source_amp * phase[:, None, :] + node_hist)
    inj1 = jnp.stack(inj_list, axis=1)
    part1 = jnp.sum(fault_colT[:, None] * inj1, axis=3).reshape(subnets, 1, steps * cases)
    part1 = jnp.concatenate(
        [part1.reshape(subnets, -1, rows), jnp.zeros((subnets, 8 - steps * cases // rows, rows), jnp.float32)], axis=1
    )
    payload1 = jnp.concatenate([inj1.reshape(subnets, steps * cases, rows), part1], axis=1)
    gathered1 = lax.all_gather(payload1, "node", axis=2, tiled=True)
    body_rows = steps * cases
    prod1 = mm("srj,scj->scr", impedance, gathered1[:, :body_rows]).reshape(subnets, steps, cases, rows)
    part_rows = steps * cases // rows
    sums1 = jnp.sum(
        gathered1[:, body_rows : body_rows + part_rows].reshape(subnets, part_rows, n_node, rows), axis=2
    ).reshape(subnets, steps, cases)
    for t in range(steps, total):
        open_v = prod1[:, t - steps]
        current = jnp.where(fault_step <= t, sums1[:, t - steps] / denominator, 0.0)
        results.append(open_v - current[:, :, None] * fault_colT)
    return jnp.stack(results)


def solution(mesh):
    in_specs = (
        P("region", "node", None),
        P("region", None, "node"),
        P("region", "node"),
        P(None, ("region", "node")),
        P(None, ("region", "node")),
        P(("region", "node")),
        P(("region", "node")),
        P(("region", "node"), None),
        P("region", None),
        P("region", None),
        P("region", None),
    )
    out_specs = P(None, "region", None, "node")
    return jax.shard_map(body, mesh=mesh, in_specs=in_specs, out_specs=out_specs, check_vma=False)
```

profile of v0, /device:TPU:0, one launch (start us, length us, event | category | flops | bytes accessed | tf_op | source)
XLA Modules:
  0.0 228.8 jit_solution(9582989218993313923)
XLA Ops:
  6.5 0.8 add_cosine_fusion.3
  7.4 8.2 %multiply_reduce_fusion.10 = (f32[2,64]{1,0:T(2,128)S(1)}, f32[2,64]{1,0:T(2,128)S(1)}, f32[2,64]{1,0:T(2,128)S(1)}, f32[2,64,256]{2,1,0:T(8,128)S(1)}, f32[2,64,256]{2,1,0:T(8,128)S(1)}, /*index=5*/f32[2,64,256]{2,1,0:T(8,128)S(1)}) fusion(s32[256]{0:T(256)S(1)} %iota_add_fusion, s32[2,64]{1,0:T(2,128)} %param.19, f32[2,64,256]{2,1,0:T(8,128)} %param.12, ...), kind=kOutput, calls=%fused_computation.170 | convolution fusion | flops 1611431552 | bytes 8920064 | tf_op jit(solution)/shard_map/srj,scj->scr/dot_general | solution.py:17
  15.6 0.7 pad_maximum_fusion.2
  16.3 0.0 all-gather.3.cloned.1.call-update
  16.4 9.6 %multiply_reduce_fusion.3 = (f32[1024]{0:T(1024)S(1)}, f32[1024]{0:T(1024)S(1)}, f32[1024]{0:T(1024)S(1)}, f32[1024]{0:T(1024)S(1)}, f32[1024]{0:T(1024)S(1)}, /...) fusion(f32[515,1024]{1,0:T(8,128)} %param.15, f32[512,1024]{1,0:T(8,128)S(1)} %copy-done.5), kind=kOutput, calls=%fused_computation.34 | convolution fusion | flops 3230130176 | bytes 12648448 | tf_op jit(solution)/shard_map/uj,jk->uk/dot_general | solution.py:17
  26.1 0.8 fusion.29
  26.9 0.2 fusion.199
  27.1 0.1 reshape.151
  27.3 0.7 broadcast_in_dim.22
  28.0 8.2 %all-to-all-start = ((f32[16,2,6,256]{3,1,2,0:T(2,128)}), f32[16,2,6,256]{3,1,2,0:T(2,128)S(1)}, u32[]{:S(2)}, u32[]{:S(2)}) async-start(f32[16,2,6,256]{3,1,2,0:T(2,128)} %broadcast_in_dim.22), calls=%async_computation | async-start | bytes 393216 | tf_op jit(solution)/shard_map/all_to_all | solution.py:71
  36.2 8.3 %all-to-all-done = f32[16,2,6,256]{3,1,2,0:T(2,128)S(1)} async-done(((f32[16,2,6,256]{3,1,2,0:T(2,128)}), f32[16,2,6,256]{3,1,2,0:T(2,128)S(1)}, u32[]{:S(2)}, u32[]{:S(2)}) %all-to-all-start) | async-done | bytes 196640 | tf_op jit(solution)/shard_map/all_to_all | solution.py:71
  44.6 0.1 reshape.153
  44.7 0.1 reshape.155
  44.8 31.6 %all-gather.3.cloned.1.call-done = f32[2,128,4096]{2,1,0:T(8,128)} async-done(((f32[2,128,256]{2,1,0:T(8,128)}), f32[2,128,4096]{2,1,0:T(8,128)}) %all-gather.3.cloned.1.call-update) | async-done | bytes 4194320 | tf_op jit(solution)/shard_map/all_gather | solution.py:59
  76.5 13.3 %fusion.18 = f32[2,132,256]{2,1,0:T(8,128)S(1)} fusion(f32[2,256,4096]{2,1,0:T(8,128)} %param.11, f32[2,4,4096]{2,1,0:T(4,128)S(1)} %reshape.153, f32[2,128,4096]{2,1,0:T(8,128)} %all-gather.3.cloned.1.call-done), kind=kOutput, calls=%fused_computation.18 | convolution fusion | flops 3322970112 | bytes 12984320 | tf_op jit(solution)/shard_map/srj,scj->scr/dot_general | solution.py:17
  89.7 0.1 bitcast_dynamic-update-slice_fusion.3
  89.8 0.1 bitcast_dynamic-update-slice_fusion.2
  89.9 0.1 bitcast_dynamic-update-slice_fusion.1
  90.0 0.1 bitcast_dynamic-update-slice_fusion
  90.1 1.2 fusion.48
  91.3 1.2 fusion.57
  92.5 1.2 fusion.66
  93.7 1.2 fusion.75
  94.9 0.1 pad_maximum_fusion
  95.0 3.3 %fusion.23 = f32[128,8,256]{2,1,0:T(8,128)} fusion(f32[256,1024,1]{1,0,2:T(8,128)S(1)} %bitcast.227, s32[1024]{0:T(1024)S(1)} %bitcast.258), kind=kOutput, calls=%fused_computation.25 | convolution fusion | flops 3222274048 | bytes 2101248 | tf_op jit(solution)/shard_map/kp,mk->pm/dot_general | solution.py:17
  98.3 7.9 %all-to-all-start.1 = ((f32[128,8,256]{2,1,0:T(8,128)}), f32[128,8,256]{2,1,0:T(8,128)S(1)}, u32[]{:S(2)}, u32[]{:S(2)}) async-start(f32[128,8,256]{2,1,0:T(8,128)} %fusion.23), calls=%async_computation.1 | async-start | bytes 2097152 | tf_op jit(solution)/shard_map/all_to_all | solution.py:97
  106.3 0.0 all-gather.5.cloned.1.call-start
  106.3 0.1 pad.4.clone
  106.4 0.9 fusion.196
  107.3 18.0 %all-to-all-done.1 = f32[128,8,256]{2,1,0:T(8,128)S(1)} async-done(((f32[128,8,256]{2,1,0:T(8,128)}), f32[128,8,256]{2,1,0:T(8,128)S(1)}, u32[]{:S(2)}, u32[]{:S(2)}) %all-to-all-start.1) | async-done | bytes 1048608 | tf_op jit(solution)/shard_map/all_to_all | solution.py:97
  125.3 3.7 %fusion.25 = f32[256,1024]{1,0:T(8,128)S(1)} fusion(s32[1024]{0:T(1024)S(1)} %bitcast.259, f32[128,8,256]{2,1,0:T(8,128)S(1)} %all-to-all-done.1), kind=kOutput, calls=%fused_computation.26 | convolution fusion | flops 3222274048 | bytes 2101248 | tf_op jit(solution)/shard_map/pm,kp->mk/dot_general | solution.py:17
  129.0 0.9 fusion.84
  129.9 0.9 fusion.93
  130.8 0.9 fusion.102
  131.8 0.9 fusion.111
  132.7 0.2 pad_maximum_fusion.1
  132.9 0.1 reshape.158
  133.0 0.9 maximum_maximum_fusion
  133.9 0.0 all-gather.5.cloned.1.call-update
  133.9 74.2 %all-gather.5.cloned.1.call-done = f32[2,264,4096]{2,1,0:T(8,128)} async-done(((f32[2,264,256]{2,1,0:T(8,128)}), f32[2,264,4096]{2,1,0:T(8,128)}) %all-gather.5.cloned.1.call-update) | async-done | bytes 8650768 | tf_op jit(solution)/shard_map/all_gather | solution.py:114
  208.2 1.0 slice_reduce_fusion.1
  209.3 0.1 reshape.161
  209.4 10.6 %fusion = f32[2,256,256]{2,1,0:T(8,128)S(1)} fusion(f32[2,256,4096]{2,1,0:T(8,128)} %param.11, f32[2,264,4096]{2,1,0:T(8,128)} %all-gather.5.cloned.1.call-done), kind=kOutput, calls=%fused_computation | convolution fusion | flops 6442450944 | bytes 17301504 | tf_op jit(solution)/shard_map/srj,scj->scr/dot_general | solution.py:17
  220.0 0.1 fusion.179
  220.1 0.1 fusion.176
  220.2 0.1 fusion.173
  220.3 1.0 copy-done.1
  221.2 0.7 fusion.170
  (40 shorter events, 0.4 us)
Async XLA Ops:
  6.5 69.9 %all-gather.3.cloned.1.call-start = ((), (), s32[]{:S(2)}) async-start(), calls=%async_computation.2 | async-start | bytes 4456448 | tf_op jit(solution)/shard_map/all_gather | solution.py:59
  7.4 9.0 %copy-start.5 = (f32[512,1024]{1,0:T(8,128)S(1)}, f32[512,1024]{1,0:T(8,128)}, u32[]{:S(2)}) copy-start(f32[512,1024]{1,0:T(8,128)} %param.14) | copy-start | bytes 6291460
  16.4 9.7 %copy-start.7 = (s32[1024]{0:T(1024)S(1)}, s32[1024]{0:T(1024)}, u32[]{:S(2)}) copy-start(s32[1024]{0:T(1024)} %param.17) | copy-start | bytes 12292
  16.4 19.8 %copy-start.3 = (f32[1024]{0:T(1024)S(1)}, f32[1024]{0:T(1024)}, u32[]{:S(2)}) copy-start(f32[1024]{0:T(1024)} %param.16) | copy-start | bytes 12292
  26.0 18.8 %copy-start.2 = (s32[2,64]{1,0:T(2,128)S(1)}, s32[2,64]{1,0:T(2,128)}, u32[]{:S(2)}) copy-start(s32[2,64]{1,0:T(2,128)} %param.20) | copy-start | bytes 1540
  26.0 18.8 %copy-start.4 = (f32[2,64]{1,0:T(2,128)S(1)}, f32[2,64]{1,0:T(2,128)}, u32[]{:S(2)}) copy-start(f32[2,64]{1,0:T(2,128)} %param.21) | copy-start | bytes 1540
  28.0 16.5 %all-to-all-start = ((f32[16,2,6,256]{3,1,2,0:T(2,128)}), f32[16,2,6,256]{3,1,2,0:T(2,128)S(1)}, u32[]{:S(2)}, u32[]{:S(2)}) async-start(f32[16,2,6,256]{3,1,2,0:T(2,128)} %broadcast_in_dim.22), calls=%async_computation | async-start | bytes 393216 | tf_op jit(solution)/shard_map/all_to_all | solution.py:71
  91.3 3.7 %copy-start.6 = (s32[1,1024]{1,0:T(1,128)S(1)}, s32[1,1024]{1,0:T(1,128)}, u32[]{:S(2)}) copy-start(s32[1,1024]{1,0:T(1,128)} %param.18) | copy-start | bytes 12292
  98.3 27.0 %all-to-all-start.1 = ((f32[128,8,256]{2,1,0:T(8,128)}), f32[128,8,256]{2,1,0:T(8,128)S(1)}, u32[]{:S(2)}, u32[]{:S(2)}) async-start(f32[128,8,256]{2,1,0:T(8,128)} %fusion.23), calls=%async_computation.1 | async-start | bytes 2097152 | tf_op jit(solution)/shard_map/all_to_all | solution.py:97
  106.3 22.7 %copy-start = (f32[2,64,256]{2,1,0:T(8,128)S(1)}, f32[2,64,256]{2,1,0:T(8,128)}, u32[]{:S(2)}) copy-start(f32[2,64,256]{2,1,0:T(8,128)} %param.12) | copy-start | bytes 393220
  106.3 101.9 %all-gather.5.cloned.1.call-start = ((), (), s32[]{:S(2)}) async-start(), calls=%async_computation.3 | async-start | bytes 9191424 | tf_op jit(solution)/shard_map/all_gather | solution.py:114
  220.3 1.0 copy-start.1
Sparse Core Ops, SparseCore 0:
  16.5 59.9 all-gather.2
  134.1 74.0 all-gather.4
where the time goes:
time: 229 us
  waiting for transfers between devices  132 us (58%)
  matrix products  58.1 us (25%)
  starting transfers between devices  16.2 us (7%)
  between operations  13.8 us (6%)
  local copies, waits for them, and re-layouts  4.35 us (2%)
  other arithmetic  4.22 us (2%)
    all_gather x1, waiting for transfers between devices, body(): gathered1 = lax.all_gather(payload1, 'node', axis=2, tiled=True)  74.2 us
    dot_general x16, matrix products, mm(): jnp.einsum(spec, a, b, precision=PRECISE, preferred_element_type=jnp.floa...  58.1 us
    all_gather x1, waiting for transfers between devices, body(): lax.all_gather(jnp.concatenate([amp_cos, amp_sin], axis=1), 'node', axis=...  31.6 us
    all_to_all x1, waiting for transfers between devices, body(): incoming = lax.all_to_all(outgoing, ('region', 'node'), 0, 0, tiled=True)  18 us
    all_to_all x1, waiting for transfers between devices, body(): small = lax.all_to_all(small, 'node', 0, 0, tiled=True)  8.3 us
    all_to_all x1, starting transfers between devices, body(): small = lax.all_to_all(small, 'node', 0, 0, tiled=True)  8.17 us
    all_to_all x1, starting transfers between devices, body(): incoming = lax.all_to_all(outgoing, ('region', 'node'), 0, 0, tiled=True)  7.94 us
  transfers between devices with their start and end apart: 4, of which 4 were waited for; matrix products, arithmetic and copies ran while one was open for 6% of the time, Pallas kernels for 0%

commit v1 on v0

--- a/solution.py
+++ b/solution.py
@@ -1,6 +1,7 @@
 import math
 
 import jax
+import numpy as np
 import jax.numpy as jnp
 from jax import lax
 from jax.sharding import PartitionSpec as P
@@ -15,6 +16,10 @@
 
 def mm(spec, a, b):
     return jnp.einsum(spec, a, b, precision=PRECISE, preferred_element_type=jnp.float32)
+
+
+def fast(spec, a, b):
+    return jnp.einsum(spec, a, b, precision=lax.Precision.HIGH, preferred_element_type=jnp.float32)
 
 
 def body(
@@ -70,42 +75,44 @@
     small = jnp.broadcast_to(small[None], (n_node,) + small.shape)
     small = lax.all_to_all(small, "node", 0, 0, tiled=True)
     h0_full = jnp.transpose(small[:, :, :steps], (1, 2, 0, 3)).reshape(subnets, steps, order)
-    prod = mm("srj,scj->scr", impedance, jnp.concatenate([sources, h0_full], axis=1))
+    prod = fast("srj,scj->scr", impedance, sources)
+    prod_h = fast("srj,stj->str", impedance, h0_full)
     sums = jnp.sum(small[:, :, steps:], axis=0).reshape(subnets, 2 * rows)
     sums = sums[:, : 7 * cases].reshape(subnets, 7, cases)
     fault_self = sums[:, 6]
     denominator = fault_self + fault_res
-
-    results = []
-    waves = []
-    for t in range(steps):
-        cw = math.cos(omega_step * t)
-        sw = math.sin(omega_step * t)
-        open_v = cw * prod[:, :cases] - sw * prod[:, cases : 2 * cases] + prod[:, 2 * cases + t][:, None, :]
-        at_fault = cw * sums[:, 0] - sw * sums[:, 1] + sums[:, 2 + t]
-        current = jnp.where(fault_step <= t, at_fault / denominator, 0.0)
-        voltage = open_v - current[:, :, None] * fault_colT
-        results.append(voltage)
-        at_ends = mm("sci,ksi->ck", voltage, attach_map.reshape(ends, subnets, rows))
-        waves.append(2.0 * conductance[None, :] * at_ends - base[t][None, :])
+    t0 = lax.iota(jnp.int32, steps)
+    cw = jnp.asarray(np.cos(omega_step * np.arange(steps)), jnp.float32)
+    sw = jnp.asarray(np.sin(omega_step * np.arange(steps)), jnp.float32)
+    open0 = (
+        cw[:, None, None, None] * prod[None, :, :cases]
+        - sw[:, None, None, None] * prod[None, :, cases:]
+        + jnp.transpose(prod_h, (1, 0, 2))[:, :, None, :]
+    )
+    fault0 = cw[:, None, None] * sums[None, :, 0] - sw[:, None, None] * sums[None, :, 1] + jnp.transpose(sums[:, 2 : 2 + steps], (1, 0, 2))
+    current0 = jnp.where(fault_step[None] <= t0[:, None, None], fault0 / denominator[None], 0.0)
+    volt0 = open0 - current0[..., None] * fault_colT[None]
+    at_ends = mm("tsci,ksi->tck", volt0, attach_map.reshape(ends, subnets, rows))
+    waves = 2.0 * conductance[None, None, :] * at_ends - base[:steps, None, :]
 
     slot_row = pair_slot[0]
     end_ids = lax.iota(jnp.int32, ends)
     selector = (end_ids[:, None] == slot_row[None, :]).astype(jnp.float32)
-    wave_block = jnp.stack(waves).reshape(steps * cases, ends)
-    outgoing = mm("kp,mk->pm", selector, wave_block)
+    outgoing = mm("kp,tck->ptc", selector, waves).reshape(ends, steps * cases)
     incoming = lax.all_to_all(outgoing, ("region", "node"), 0, 0, tiled=True)
     far = mm("pm,kp->mk", incoming, selector).reshape(steps, cases, ends)
 
-    inj_list = []
+    hist_list = []
     for t in range(steps, total):
         history = base[t][None, :]
         for j in range(t - steps + 1):
             history = history + impulse_taps[j][None, :] * far[t - steps - j]
-        node_hist = mm("ck,ksi->sci", history, attach_map.reshape(ends, subnets, rows))
-        phase = jnp.cos(omega_step * t + source_angle)
-        inj_list.append(source_amp * phase[:, None, :] + node_hist)
-    inj1 = jnp.stack(inj_list, axis=1)
+        hist_list.append(history)
+    node_hist = mm("tck,ksi->stci", jnp.stack(hist_list), attach_map.reshape(ends, subnets, rows))
+    t1 = lax.iota(jnp.int32, steps) + steps
+    angle1 = jnp.asarray(omega_step * np.arange(steps, total), jnp.float32)
+    phase = jnp.cos(angle1[None, :, None] + source_angle[:, None, :])
+    inj1 = source_amp[:, None] * phase[:, :, None, :] + node_hist
     part1 = jnp.sum(fault_colT[:, None] * inj1, axis=3).reshape(subnets, 1, steps * cases)
     part1 = jnp.concatenate(
         [part1.reshape(subnets, -1, rows), jnp.zeros((subnets, 8 - steps * cases // rows, rows), jnp.float32)], axis=1
@@ -113,16 +120,14 @@
     payload1 = jnp.concatenate([inj1.reshape(subnets, steps * cases, rows), part1], axis=1)
     gathered1 = lax.all_gather(payload1, "node", axis=2, tiled=True)
     body_rows = steps * cases
-    prod1 = mm("srj,scj->scr", impedance, gathered1[:, :body_rows]).reshape(subnets, steps, cases, rows)
+    prod1 = fast("srj,scj->scr", impedance, gathered1[:, :body_rows]).reshape(subnets, steps, cases, rows)
     part_rows = steps * cases // rows
     sums1 = jnp.sum(
         gathered1[:, body_rows : body_rows + part_rows].reshape(subnets, part_rows, n_node, rows), axis=2
     ).reshape(subnets, steps, cases)
-    for t in range(steps, total):
-        open_v = prod1[:, t - steps]
-        current = jnp.where(fault_step <= t, sums1[:, t - steps] / denominator, 0.0)
-        results.append(open_v - current[:, :, None] * fault_colT)
-    return jnp.stack(results)
+    current1 = jnp.where(fault_step[None] <= t1[:, None, None], jnp.transpose(sums1, (1, 0, 2)) / denominator[None], 0.0)
+    volt1 = jnp.transpose(prod1, (1, 0, 2, 3)) - current1[..., None] * fault_colT[None]
+    return jnp.concatenate([volt0, volt1], axis=0)
 
 
 def solution(mesh):

time: 229 us -> 222 us (0.969)
  waiting for transfers between devices: 132 us -> 121 us
  local copies, waits for them, and re-layouts: 4.35 us -> 7.19 us
  matrix products: 58.1 us -> 60.4 us
    dot_general x0 -> x3, matrix products: none -> 29.1 us  [fast(): jnp.einsum(spec, a, b, precision=lax.Precision.HIGH, preferred_element_ty...]
    dot_general x16 -> x8, matrix products: 58.1 us -> 31.3 us  [mm(): jnp.einsum(spec, a, b, precision=PRECISE, preferred_element_type=jnp.floa...]
    all_gather x1, waiting for transfers between devices: 31.6 us -> 20.8 us  [body(): lax.all_gather(jnp.concatenate([amp_cos, amp_sin], axis=1), 'node', axis=...]
  transfers between devices with their start and end apart: 4 -> 4, of which waited for: 4 -> 4; matrix products, arithmetic and copies ran while one was open for 6% -> 11% of each run, Pallas kernels for 0% -> 0%
where the time goes in v1:
time: 222 us
  waiting for transfers between devices  121 us (55%)
  matrix products  60.4 us (27%)
  starting transfers between devices  15.9 us (7%)
  between operations  13.9 us (6%)
  local copies, waits for them, and re-layouts  7.19 us (3%)
  other arithmetic  3.54 us (2%)
    all_gather x1, waiting for transfers between devices, body(): gathered1 = lax.all_gather(payload1, 'node', axis=2, tiled=True)  74.2 us
    dot_general x8, matrix products, mm(): jnp.einsum(spec, a, b, precision=PRECISE, preferred_element_type=jnp.floa...  31.3 us
    dot_general x3, matrix products, fast(): jnp.einsum(spec, a, b, precision=lax.Precision.HIGH, preferred_element_ty...  29.1 us
    all_gather x1, waiting for transfers between devices, body(): lax.all_gather(jnp.concatenate([amp_cos, amp_sin], axis=1), 'node', axis=...  20.8 us
    all_to_all x1, waiting for transfers between devices, body(): incoming = lax.all_to_all(outgoing, ('region', 'node'), 0, 0, tiled=True)  17.5 us
    all_to_all x1, waiting for transfers between devices, body(): small = lax.all_to_all(small, 'node', 0, 0, tiled=True)  8.09 us
    all_to_all x1, starting transfers between devices, body(): small = lax.all_to_all(small, 'node', 0, 0, tiled=True)  8 us
    all_to_all x1, starting transfers between devices, body(): incoming = lax.all_to_all(outgoing, ('region', 'node'), 0, 0, tiled=True)  7.63 us
  transfers between devices with their start and end apart: 4, of which 4 were waited for; matrix products, arithmetic and copies ran while one was open for 11% of the time, Pallas kernels for 0%

profile of v1, /device:TPU:0, one launch (start us, length us, event | category | flops | bytes accessed | tf_op | source)
XLA Modules:
  0.0 221.6 jit_solution(10587389721224576368)
XLA Ops:
  6.5 0.7 fusion.43
  7.3 8.0 %multiply_reduce_fusion.10 = (f32[2,64]{1,0:T(2,128)S(1)}, f32[2,64]{1,0:T(2,128)S(1)}, f32[2,64]{1,0:T(2,128)S(1)}, f32[2,64,256]{2,1,0:T(8,128)S(1)}, f32[2,64,256]{2,1,0:T(8,128)S(1)}, /*index=5*/f32[2,64,256]{2,1,0:T(8,128)S(1)}) fusion(s32[256]{0:T(256)S(1)} %iota_add_fusion, s32[2,64]{1,0:T(2,128)} %param.22, f32[2,64,256]{2,1,0:T(8,128)} %param.15, ...), kind=kOutput, calls=%fused_computation.65 | convolution fusion | flops 1611431552 | bytes 8920064 | tf_op jit(solution)/shard_map/srj,scj->scr/dot_general | solution.py:18
  15.3 0.7 pad_maximum_fusion.1
  16.0 0.0 all-gather.3.cloned.1.call-update
  16.1 0.0 copy-start.15
  16.1 0.0 copy-start.7
  16.1 0.0 copy-start.9
  16.1 0.0 copy-start.11
  16.1 13.7 %multiply_reduce_fusion.3 = (f32[1024]{0:T(1024)}, f32[1024]{0:T(1024)}, f32[1024]{0:T(1024)}, f32[1024]{0:T(1024)}, f32[1024]{0:T(1024)S(1)}, /*index=5*/f32[1024]{0:T(1024)S(1)}, f32[1024]{0:T(1024)S(1)}, f32[1024]{0:T(1024)S(1)}) fusion(f32[515,1024]{1,0:T(8,128)} %param.18, f32[512,1024]{1,0:T(8,128)} %param.17), kind=kOutput, calls=%fused_computation.15 | convolution fusion | flops 3230130176 | bytes 12648448 | tf_op jit(solution)/shard_map/uj,jk->uk/dot_general | solution.py:18
  29.9 0.8 fusion.11
  30.7 0.2 fusion.45
  30.9 0.1 reshape.102
  31.0 0.7 broadcast_in_dim.17
  31.8 8.0 %all-to-all-start = ((f32[16,2,6,256]{3,1,2,0:T(2,128)}), f32[16,2,6,256]{3,1,2,0:T(2,128)S(1)}, u32[]{:S(2)}, u32[]{:S(2)}) async-start(f32[16,2,6,256]{3,1,2,0:T(2,128)} %broadcast_in_dim.17), calls=%async_computation | async-start | bytes 393216 | tf_op jit(solution)/shard_map/all_to_all | solution.py:76
  39.8 8.1 %all-to-all-done = f32[16,2,6,256]{3,1,2,0:T(2,128)S(1)} async-done(((f32[16,2,6,256]{3,1,2,0:T(2,128)}), f32[16,2,6,256]{3,1,2,0:T(2,128)S(1)}, u32[]{:S(2)}, u32[]{:S(2)}) %all-to-all-start) | async-done | bytes 196640 | tf_op jit(solution)/shard_map/all_to_all | solution.py:76
  48.0 0.1 reshape.106
  48.1 0.1 divide_select_fusion
  48.2 0.1 reshape.104
  48.3 6.9 %convolution_bitcast_fusion = f32[4,2,256]{2,0,1:T(4,128)S(1)} fusion(f32[2,4,4096]{2,1,0:T(4,128)S(1)} %reshape.104, f32[2,256,4096]{2,1,0:T(8,128)} %param.14), kind=kOutput, calls=%fused_computation.29 | convolution fusion | flops 50331648 | bytes 8527872 | tf_op jit(solution)/shard_map/srj,stj->str/dot_general | solution.py:22
  55.2 20.8 %all-gather.3.cloned.1.call-done = f32[2,128,4096]{2,1,0:T(8,128)} async-done(((f32[2,128,256]{2,1,0:T(8,128)}), f32[2,128,4096]{2,1,0:T(8,128)}) %all-gather.3.cloned.1.call-update) | async-done | bytes 4194320 | tf_op jit(solution)/shard_map/all_gather | solution.py:64
  76.0 8.9 %fusion.44 = f32[2,128,256]{2,1,0:T(8,128)S(1)} fusion(f32[2,128,4096]{2,1,0:T(8,128)} %all-gather.3.cloned.1.call-done, f32[2,256,4096]{2,1,0:T(8,128)} %param.14), kind=kOutput, calls=%fused_computation.90 | convolution fusion | flops 1610612736 | bytes 12845056 | tf_op jit(solution)/shard_map/srj,scj->scr/dot_general | solution.py:22
  84.9 0.0 copy-start.17
  85.0 1.4 fusion.14
  86.3 2.2 fusion.4
  88.5 0.9 copy.59
  89.4 0.0 copy-start.1
  89.4 0.0 copy-start.16
  89.5 2.1 all_to_all.12
  91.6 7.6 %all-to-all-start.1 = ((f32[128,8,256]{2,1,0:T(8,128)}), f32[128,8,256]{2,1,0:T(8,128)S(1)}, u32[]{:S(2)}, u32[]{:S(2)}) async-start(f32[128,8,256]{2,1,0:T(8,128)} %all_to_all.12), calls=%async_computation.1 | async-start | bytes 2097152 | tf_op jit(solution)/shard_map/all_to_all | solution.py:102
  99.2 0.3 all-gather.5.cloned.1.call-start
  99.5 0.1 pad.6.clone
  99.6 0.1 add_cosine_fusion
  99.7 0.9 fusion.40
  100.7 0.0 copy-start
  100.7 17.5 %all-to-all-done.1 = f32[128,8,256]{2,1,0:T(8,128)S(1)} async-done(((f32[128,8,256]{2,1,0:T(8,128)}), f32[128,8,256]{2,1,0:T(8,128)S(1)}, u32[]{:S(2)}, u32[]{:S(2)}) %all-to-all-start.1) | async-done | bytes 1048608 | tf_op jit(solution)/shard_map/all_to_all | solution.py:102
  118.2 3.7 %fusion.2 = f32[256,1024]{1,0:T(8,128)S(1)} fusion(s32[1024]{0:T(1024)S(1)} %bitcast.136, f32[128,8,256]{2,1,0:T(8,128)S(1)} %all-to-all-done.1), kind=kOutput, calls=%fused_computation.3 | convolution fusion | flops 3222274048 | bytes 2101248 | tf_op jit(solution)/shard_map/pm,kp->mk/dot_general | solution.py:18
  121.9 0.2 add_bitcast_fusion
  122.2 1.4 multiply_reduce_fusion.8
  123.6 0.1 reshape.108
  123.7 0.9 maximum_maximum_fusion
  124.6 0.0 all-gather.5.cloned.1.call-update
  124.6 74.2 %all-gather.5.cloned.1.call-done = f32[2,264,4096]{2,1,0:T(8,128)} async-done(((f32[2,264,256]{2,1,0:T(8,128)}), f32[2,264,4096]{2,1,0:T(8,128)}) %all-gather.5.cloned.1.call-update) | async-done | bytes 8650768 | tf_op jit(solution)/shard_map/all_gather | solution.py:121
  198.8 1.0 slice_reduce_fusion.1
  199.9 0.1 reshape.111
  200.0 0.1 bitcast_select_fusion
  200.1 13.3 %fusion = f32[2,256,256]{2,1,0:T(8,128)S(1)} fusion(f32[2,256,4096]{2,1,0:T(8,128)} %param.14, f32[2,264,4096]{2,1,0:T(8,128)} %all-gather.5.cloned.1.call-done), kind=kOutput, calls=%fused_computation | convolution fusion | flops 3221225472 | bytes 17301504 | tf_op jit(solution)/shard_map/srj,scj->scr/dot_general | solution.py:22
  213.4 0.2 multiply_subtract_fusion
  213.7 1.1 pad_maximum_fusion
  (57 shorter events, 0.4 us)
Async XLA Ops:
  6.5 69.4 %all-gather.3.cloned.1.call-start = ((), (), s32[]{:S(2)}) async-start(), calls=%async_computation.2 | async-start | bytes 4456448 | tf_op jit(solution)/shard_map/all_gather | solution.py:64
  16.1 13.8 %copy-start.19 = (s32[1024]{0:T(1024)S(1)}, s32[1024]{0:T(1024)}, u32[]{:S(2)}) copy-start(s32[1024]{0:T(1024)} %param.20) | copy-start | bytes 12292
  16.1 23.7 %copy-start.6 = (f32[1024]{0:T(1024)S(1)}, f32[1024]{0:T(1024)}, u32[]{:S(2)}) copy-start(f32[1024]{0:T(1024)} %param.19) | copy-start | bytes 12292
  16.1 32.0 %copy-start.15 = (f32[2,64]{1,0:T(2,128)S(1)}, f32[2,64]{1,0:T(2,128)}, u32[]{:S(2)}) copy-start(f32[2,64]{1,0:T(2,128)} %param.24) | copy-start | bytes 1540
  16.1 32.0 %copy-start.7 = (s32[2,64]{1,0:T(2,128)S(1)}, s32[2,64]{1,0:T(2,128)}, u32[]{:S(2)}) copy-start(s32[2,64]{1,0:T(2,128)} %param.23) | copy-start | bytes 1540
  16.1 31.9 %copy-start.9 = (f32[4]{0:T(128)S(1)}, f32[4]{0:T(128)}, u32[]{:S(2)}) copy-start(f32[4]{0:T(128)} %constant.26.clone) | copy-start | bytes 52
  16.1 31.9 %copy-start.11 = (f32[4]{0:T(128)S(1)}, f32[4]{0:T(128)}, u32[]{:S(2)}) copy-start(f32[4]{0:T(128)} %constant.8.clone) | copy-start | bytes 52
  31.8 16.2 %all-to-all-start = ((f32[16,2,6,256]{3,1,2,0:T(2,128)}), f32[16,2,6,256]{3,1,2,0:T(2,128)S(1)}, u32[]{:S(2)}, u32[]{:S(2)}) async-start(f32[16,2,6,256]{3,1,2,0:T(2,128)} %broadcast_in_dim.17), calls=%async_computation | async-start | bytes 393216 | tf_op jit(solution)/shard_map/all_to_all | solution.py:76
  39.8 45.2 %copy-start.13 = (s32[2,256]{1,0:T(2,128)}, s32[2,256]{1,0:T(2,128)S(1)}, u32[]{:S(2)}) copy-start(s32[2,256]{1,0:T(2,128)S(1)} %multiply_add_fusion) | copy-start | bytes 6148
  84.9 1.4 copy-start.17
  89.4 10.2 %copy-start.1 = (f32[2,256]{1,0:T(2,128)S(1)}, f32[2,256]{1,0:T(2,128)}, u32[]{:S(2)}) copy-start(f32[2,256]{1,0:T(2,128)} %param.16) | copy-start | bytes 6148
  89.4 10.2 %copy-start.16 = (f32[4]{0:T(128)S(1)}, f32[4]{0:T(128)}, u32[]{:S(2)}) copy-start(f32[4]{0:T(128)} %constant.27.clone) | copy-start | bytes 52
  89.4 28.8 %copy-start.18 = (s32[1,1024]{1,0:T(1,128)S(1)}, s32[1,1024]{1,0:T(1,128)}, u32[]{:S(2)}) copy-start(s32[1,1024]{1,0:T(1,128)} %param.21) | copy-start | bytes 12292
  91.6 26.7 %all-to-all-start.1 = ((f32[128,8,256]{2,1,0:T(8,128)}), f32[128,8,256]{2,1,0:T(8,128)S(1)}, u32[]{:S(2)}, u32[]{:S(2)}) async-start(f32[128,8,256]{2,1,0:T(8,128)} %all_to_all.12), calls=%async_computation.1 | async-start | bytes 2097152 | tf_op jit(solution)/shard_map/all_to_all | solution.py:102
  99.2 22.7 %copy-start.2 = (f32[1024]{0:T(1024)S(1)}, f32[1024]{0:T(1024)}, u32[]{:S(2)}) copy-start(f32[1024]{0:T(1024)} %get-tuple-element.5) | copy-start | bytes 12292
  99.2 22.7 %copy-start.3 = (f32[1024]{0:T(1024)S(1)}, f32[1024]{0:T(1024)}, u32[]{:S(2)}) copy-start(f32[1024]{0:T(1024)} %get-tuple-element.6) | copy-start | bytes 12292
  99.2 22.7 %copy-start.4 = (f32[1024]{0:T(1024)S(1)}, f32[1024]{0:T(1024)}, u32[]{:S(2)}) copy-start(f32[1024]{0:T(1024)} %get-tuple-element.7) | copy-start | bytes 12292
  99.2 22.7 %copy-start.5 = (f32[1024]{0:T(1024)S(1)}, f32[1024]{0:T(1024)}, u32[]{:S(2)}) copy-start(f32[1024]{0:T(1024)} %get-tuple-element.8) | copy-start | bytes 12292
  99.2 99.6 %all-gather.5.cloned.1.call-start = ((), (), s32[]{:S(2)}) async-start(), calls=%async_computation.3 | async-start | bytes 9191424 | tf_op jit(solution)/shard_map/all_gather | solution.py:121
  100.7 21.5 %copy-start = (f32[2,64,256]{2,1,0:T(8,128)S(1)}, f32[2,64,256]{2,1,0:T(8,128)}, u32[]{:S(2)}) copy-start(f32[2,64,256]{2,1,0:T(8,128)} %param.15) | copy-start | bytes 393220
  100.7 21.5 %copy-start.14 = (s32[2,256]{1,0:T(2,128)S(1)}, s32[2,256]{1,0:T(2,128)}, u32[]{:S(2)}) copy-start(s32[2,256]{1,0:T(2,128)} %copy-done.13) | copy-start | bytes 6148
  100.7 21.5 %copy-start.20 = (s32[1024]{0:T(1024)S(1)}, s32[1024]{0:T(1024)}, u32[]{:S(2)}) copy-start(s32[1024]{0:T(1024)} %param.20) | copy-start | bytes 12292
  122.2 77.8 %copy-start.8 = (s32[2,64]{1,0:T(2,128)S(1)}, s32[2,64]{1,0:T(2,128)}, u32[]{:S(2)}) copy-start(s32[2,64]{1,0:T(2,128)} %param.23) | copy-start | bytes 1540
  200.1 13.3 %copy-start.10 = (f32[4]{0:T(128)S(1)}, f32[4]{0:T(128)}, u32[]{:S(2)}) copy-start(f32[4]{0:T(128)} %constant.26.clone) | copy-start | bytes 52
  200.1 13.3 %copy-start.12 = (f32[4]{0:T(128)S(1)}, f32[4]{0:T(128)}, u32[]{:S(2)}) copy-start(f32[4]{0:T(128)} %constant.8.clone) | copy-start | bytes 52
Sparse Core Ops, SparseCore 0:
  16.2 59.7 all-gather.2
  124.7 74.0 all-gather.4

commit v2 on v1

v2 whole, which is shorter than its diff:
```python
import math

import jax
import numpy as np
import jax.numpy as jnp
from jax import lax
from jax.sharding import PartitionSpec as P

WINDOW_STEPS = 4
WINDOW_COUNT = 2


omega_step = 2.0 * math.pi / 400.0
PRECISE = lax.Precision.HIGHEST


def mm(spec, a, b):
    return jnp.einsum(spec, a, b, precision=PRECISE, preferred_element_type=jnp.float32)


def fast(spec, a, b):
    return jnp.einsum(spec, a, b, precision=lax.Precision.HIGH, preferred_element_type=jnp.float32)


def body(
    impedance,
    source_amp,
    source_angle,
    impulse_taps,
    incident,
    conductance,
    attach,
    pair_slot,
    fault_node,
    fault_step,
    fault_res,
):
    subnets, rows, order = impedance.shape
    cases = source_amp.shape[1]
    tap_len, ends = impulse_taps.shape
    past = incident.shape[0]
    steps = WINDOW_STEPS
    total = WINDOW_STEPS * WINDOW_COUNT
    n_node = order // rows
    local = subnets * rows
    row_ids = lax.axis_index("node") * rows + lax.iota(jnp.int32, rows)

    amp_t = jnp.transpose(source_amp, (0, 2, 1))
    amp_cos = amp_t * jnp.cos(source_angle)[:, :, None]
    amp_sin = amp_t * jnp.sin(source_angle)[:, :, None]
    amp_cos, amp_sin = lax.optimization_barrier((amp_cos, amp_sin))
    sources = lax.all_gather(jnp.concatenate([amp_cos, amp_sin], axis=2), "node", axis=1, tiled=True)

    local_ids = lax.iota(jnp.int32, local)
    attach_map = (attach[:, None] == local_ids[None, :]).astype(jnp.float32)
    attach_mapT = (local_ids[:, None] == attach[None, :]).astype(jnp.float32)

    onehotT = (lax.iota(jnp.int32, order)[None, :, None] == fault_node[:, None, :]).astype(jnp.float32)
    fault_col = mm("srj,sjc->src", impedance, onehotT)
    owner = (row_ids[None, :, None] == fault_node[:, None, :]).astype(jnp.float32)
    self_part = jnp.sum(fault_col * owner, axis=1)

    flip = (lax.iota(jnp.int32, tap_len)[:, None] + lax.iota(jnp.int32, tap_len)[None, :] == tap_len - 1).astype(
        jnp.float32
    )
    taps_rev = mm("uj,jk->uk", flip, impulse_taps)
    padded = jnp.concatenate([incident, jnp.zeros((tap_len + total - 1 - past, ends), jnp.float32)], axis=0)
    base = jnp.stack([jnp.sum(taps_rev * padded[t : t + tap_len], axis=0) for t in range(total)])
    base_node = mm("tk,kn->tn", base[:steps], attach_map).reshape(steps, subnets, rows)
    h0 = jnp.transpose(base_node, (1, 0, 2))

    part_cos = jnp.sum(fault_col * amp_cos, axis=1)
    part_sin = jnp.sum(fault_col * amp_sin, axis=1)
    part_h = mm("sic,sti->stc", fault_col, h0)
    partials = jnp.concatenate(
        [part_cos[:, None], part_sin[:, None], part_h, self_part[:, None]], axis=1
    ).reshape(subnets, -1)
    pad_len = 2 * rows - partials.shape[1]
    partials = jnp.concatenate([partials, jnp.zeros((subnets, pad_len), jnp.float32)], axis=1)
    small = jnp.concatenate([h0, partials.reshape(subnets, 2, rows)], axis=1)
    small = jnp.broadcast_to(small[None], (n_node,) + small.shape)
    small = lax.all_to_all(small, "node", 0, 0, tiled=True)
    h0_full = jnp.transpose(small[:, :, :steps], (1, 0, 3, 2)).reshape(subnets, order, steps)
    sums = jnp.sum(small[:, :, steps:], axis=0).reshape(subnets, 2 * rows)
    sums = sums[:, : 7 * cases].reshape(subnets, 7, cases)
    denominator = sums[:, 6] + fault_res

    prod = fast("srj,sjc->src", impedance, sources)
    prod_h = fast("srj,sjt->srt", impedance, h0_full)
    t0 = lax.iota(jnp.int32, steps)
    cw = jnp.asarray(np.cos(omega_step * np.arange(steps)), jnp.float32)
    sw = jnp.asarray(np.sin(omega_step * np.arange(steps)), jnp.float32)
    open0 = (
        cw[None, None, :, None] * prod[:, :, None, :cases]
        - sw[None, None, :, None] * prod[:, :, None, cases:]
        + prod_h[:, :, :, None]
    )
    fault0 = cw[None, :, None] * sums[:, 0][:, None] - sw[None, :, None] * sums[:, 1][:, None] + sums[:, 2 : 2 + steps]
    current0 = jnp.where(fault_step[:, None, :] <= t0[None, :, None], fault0 / denominator[:, None, :], 0.0)
    volt0 = open0 - current0[:, None] * fault_col[:, :, None, :]

    at_ends = mm("kn,nm->km", attach_map, volt0.reshape(local, steps * cases)).reshape(ends, steps, cases)
    waves = 2.0 * conductance[:, None, None] * at_ends - jnp.transpose(base[:steps])[:, :, None]

    slot_row = pair_slot[0]
    end_ids = lax.iota(jnp.int32, ends)
    selector = (end_ids[:, None] == slot_row[None, :]).astype(jnp.float32)
    selectorT = (slot_row[:, None] == end_ids[None, :]).astype(jnp.float32)
    outgoing = mm("pk,km->pm", selectorT, waves.reshape(ends, steps * cases))
    incoming = lax.all_to_all(outgoing, ("region", "node"), 0, 0, tiled=True)
    far = mm("kp,pm->km", selector, incoming).reshape(ends, steps, cases)

    taps_t = jnp.transpose(impulse_taps[:steps])
    base_t = jnp.transpose(base[steps:])
    hist_list = []
    for t in range(steps, total):
        history = base_t[:, t - steps][:, None]
        for j in range(t - steps + 1):
            history = history + taps_t[:, j][:, None] * far[:, t - steps - j]
        hist_list.append(history)
    hist1 = jnp.stack(hist_list, axis=1).reshape(ends, steps * cases)
    node_hist = mm("nk,km->nm", attach_mapT, hist1).reshape(subnets, rows, steps, cases)
    angle1 = jnp.asarray(omega_step * np.arange(steps, total), jnp.float32)
    phase = jnp.cos(angle1[None, None, :] + source_angle[:, :, None])
    inj1 = amp_t[:, :, None, :] * phase[:, :, :, None] + node_hist
    part1 = jnp.sum(fault_col[:, :, None, :] * inj1, axis=1)
    part1 = lax.all_to_all(jnp.broadcast_to(part1[None], (n_node,) + part1.shape), "node", 0, 0, tiled=True)
    sums1 = jnp.sum(part1, axis=0)
    gathered1 = lax.all_gather(inj1.reshape(subnets, rows, steps * cases), "node", axis=1, tiled=True)
    prod1 = fast("srj,sjm->srm", impedance, gathered1).reshape(subnets, rows, steps, cases)
    t1 = t0 + steps
    current1 = jnp.where(fault_step[:, None, :] <= t1[None, :, None], sums1 / denominator[:, None, :], 0.0)
    volt1 = prod1 - current1[:, None] * fault_col[:, :, None, :]
    volt = jnp.concatenate([volt0, volt1], axis=2)
    return jnp.transpose(volt, (2, 0, 3, 1))


def solution(mesh):
    in_specs = (
        P("region", "node", None),
        P("region", None, "node"),
        P("region", "node"),
        P(None, ("region", "node")),
        P(None, ("region", "node")),
        P(("region", "node")),
        P(("region", "node")),
        P(("region", "node"), None),
        P("region", None),
        P("region", None),
        P("region", None),
    )
    out_specs = P(None, "region", None, "node")
    return jax.shard_map(body, mesh=mesh, in_specs=in_specs, out_specs=out_specs, check_vma=False)
```

time: 222 us -> 211 us (0.950)
  waiting for transfers between devices: 121 us -> 108 us
  starting transfers between devices: 15.9 us -> 19.6 us
  matrix products: 60.4 us -> 57.4 us
    all_gather x2, waiting for transfers between devices: 95 us -> 76.3 us  [the longest x1 59.8 us: body(): lax.all_gather(inj1.reshape(subnets, rows, steps * cases), 'node', axis=1...]
    all_to_all x0 -> x1, waiting for transfers between devices: none -> 7.56 us  [body(): lax.all_to_all(jnp.broadcast_to(part1[None], (n_node,) + part1.shape), 'n...]
    all_to_all x0 -> x1, starting transfers between devices: none -> 3.48 us  [body(): lax.all_to_all(jnp.broadcast_to(part1[None], (n_node,) + part1.shape), 'n...]
    dot_general x8, matrix products: 31.3 us -> 28.3 us  [mm(): jnp.einsum(spec, a, b, precision=PRECISE, preferred_element_type=jnp.floa...]
    all_to_all x1, waiting for transfers between devices: 8.09 us -> 5.69 us  [body(): small = lax.all_to_all(small, 'node', 0, 0, tiled=True)]
  transfers between devices with their start and end apart: 4 -> 5, of which waited for: 4 -> 5; matrix products, arithmetic and copies ran while one was open for 11% -> 15% of each run, Pallas kernels for 0% -> 0%
where the time goes in v2:
time: 211 us
  waiting for transfers between devices  108 us (51%)
  matrix products  57.4 us (27%)
  starting transfers between devices  19.6 us (9%)
  between operations  13.9 us (7%)
  local copies, waits for them, and re-layouts  7.5 us (4%)
  other arithmetic  4.76 us (2%)
    all_gather x1, waiting for transfers between devices, body(): lax.all_gather(inj1.reshape(subnets, rows, steps * cases), 'node', axis=1...  59.8 us
    dot_general x3, matrix products, fast(): jnp.einsum(spec, a, b, precision=lax.Precision.HIGH, preferred_element_ty...  29 us
    dot_general x8, matrix products, mm(): jnp.einsum(spec, a, b, precision=PRECISE, preferred_element_type=jnp.floa...  28.3 us
    all_to_all x1, waiting for transfers between devices, body(): incoming = lax.all_to_all(outgoing, ('region', 'node'), 0, 0, tiled=True)  18 us
    all_gather x1, waiting for transfers between devices, body(): lax.all_gather(jnp.concatenate([amp_cos, amp_sin], axis=2), 'node', axis=...  16.5 us
    all_to_all x1, starting transfers between devices, body(): small = lax.all_to_all(small, 'node', 0, 0, tiled=True)  8.17 us
    all_to_all x1, starting transfers between devices, body(): incoming = lax.all_to_all(outgoing, ('region', 'node'), 0, 0, tiled=True)  7.94 us
    all_to_all x1, waiting for transfers between devices, body(): lax.all_to_all(jnp.broadcast_to(part1[None], (n_node,) + part1.shape), 'n...  7.56 us
  transfers between devices with their start and end apart: 5, of which 5 were waited for; matrix products, arithmetic and copies ran while one was open for 15% of the time, Pallas kernels for 0%

profile of v2, /device:TPU:0, one launch (start us, length us, event | category | flops | bytes accessed | tf_op | source)
XLA Modules:
  0.0 210.8 jit_solution(13588419102340418138)
XLA Ops:
  6.5 0.7 fusion.49
  7.3 0.9 broadcast_multiply_fusion.1
  8.2 0.7 pad_maximum_fusion
  9.0 13.2 %multiply_reduce_fusion.3 = (f32[1024]{0:T(1024)S(1)}, f32[1024]{0:T(1024)S(1)}, f32[1024]{0:T(1024)S(1)}, f32[1024]{0:T(1024)S(1)}, f32[1024]{0:T(1024)S(1)}, /...) fusion(f32[515,1024]{1,0:T(8,128)} %param.18, f32[512,1024]{1,0:T(8,128)} %param.17), kind=kOutput, calls=%fused_computation.11 | convolution fusion | flops 3230130176 | bytes 12648448 | tf_op jit(solution)/shard_map/uj,jk->uk/dot_general | solution.py:18
  22.2 0.8 fusion.8
  23.1 4.7 %multiply_reduce_fusion.10 = (f32[2,64]{1,0:T(2,128)S(1)}, f32[2,64]{1,0:T(2,128)S(1)}, f32[2,64]{1,0:T(2,128)S(1)}, f32[2,64,256]{2,1,0:T(8,128)S(1)}) fusion(f32[2,256,64]{1,2,0:T(8,128)S(1)} %get-tuple-element.7, f32[2,256,64]{1,2,0:T(8,128)S(1)} %get-tuple-element.8, s32[2,64]{1,0:T(2,128)S(1)} %copy-done.7, s32[256]{0:T(256)S(1)} %iota_add_fusion, ...), kind=kOutput, calls=%fused_computation.63 | convolution fusion | flops 1611366016 | bytes 8784896 | tf_op jit(solution)/shard_map/srj,sjc->src/dot_general | solution.py:18
  27.8 0.2 fusion.50
  28.2 0.7 broadcast_in_dim.17
  28.9 8.2 %all-to-all-start = ((f32[16,2,6,256]{3,1,2,0:T(2,128)}), f32[16,2,6,256]{3,1,2,0:T(2,128)S(1)}, u32[]{:S(2)}, u32[]{:S(2)}) async-start(f32[16,2,6,256]{3,1,2,0:T(2,128)} %broadcast_in_dim.17), calls=%async_computation | async-start | bytes 393216 | tf_op jit(solution)/shard_map/all_to_all | solution.py:82
  37.2 0.1 mul.311
  37.3 0.1 mul.316
  37.4 0.5 broadcast.175
  37.9 0.6 reduce.3
  38.5 0.1 eq.136
  38.7 0.7 fusion.3
  39.4 5.7 %all-to-all-done = f32[16,2,6,256]{3,1,2,0:T(2,128)S(1)} async-done(((f32[16,2,6,256]{3,1,2,0:T(2,128)}), f32[16,2,6,256]{3,1,2,0:T(2,128)S(1)}, u32[]{:S(2)}, u32[]{:S(2)}) %all-to-all-start) | async-done | bytes 196640 | tf_op jit(solution)/shard_map/all_to_all | solution.py:82
  45.4 6.8 %convolution_bitcast_fusion.1 = f32[2,256,4]{1,2,0:T(4,128)S(1)} fusion(f32[2,4096,4]{1,2,0:T(4,128)S(1)} %reshape.215, f32[2,256,4096]{2,1,0:T(8,128)} %param.14), kind=kOutput, calls=%fused_computation.29 | convolution fusion | flops 50331648 | bytes 8527872 | tf_op jit(solution)/shard_map/srj,sjt->srt/dot_general | solution.py:22
  52.2 0.1 add.142.clone
  52.5 16.5 %all-gather.3.cloned.1.call-done = f32[2,4096,128]{1,2,0:T(8,128)} async-done(((f32[2,256,128]{1,2,0:T(8,128)}), f32[2,4096,128]{1,2,0:T(8,128)}) %all-gather.3.cloned.1.call-update) | async-done | bytes 4194320 | tf_op jit(solution)/shard_map/all_gather | solution.py:52
  68.9 8.9 %convolution_bitcast_fusion = f32[2,256,128]{1,2,0:T(8,128)S(1)} fusion(f32[2,4096,128]{1,2,0:T(8,128)} %all-gather.3.cloned.1.call-done, f32[2,256,4096]{2,1,0:T(8,128)} %param.14), kind=kOutput, calls=%fused_computation.28 | convolution fusion | flops 1610612736 | bytes 12845056 | tf_op jit(solution)/shard_map/srj,sjc->src/dot_general | solution.py:22
  77.9 0.1 copy.118
  78.0 0.1 copy.119
  78.1 0.2 add_subtract_fusion.1
  78.3 0.4 copy.106
  78.8 0.1 mul.275.clone
  79.0 0.1 mul.278.clone
  79.2 0.2 add_subtract_fusion
  79.3 1.3 fusion.18
  80.6 4.0 %fusion.4 = f32[128,8,256]{2,1,0:T(8,128)} fusion(f32[1024,256,1]{0,1,2:T(8,128)S(1)} %bitcast.187, pred[128,8,1024]{2,0,1:T(32,128)(4,1)S(1)} %fusion.3), kind=kOutput, calls=%fused_computation.5 | convolution fusion | flops 3221225472 | bytes 3145728 | tf_op jit(solution)/shard_map/pk,km->pm/dot_general | solution.py:18
  84.6 7.9 %all-to-all-start.1 = ((f32[128,8,256]{2,1,0:T(8,128)}), f32[128,8,256]{2,1,0:T(8,128)S(1)}, u32[]{:S(2)}, u32[]{:S(2)}) async-start(f32[128,8,256]{2,1,0:T(8,128)} %fusion.4), calls=%async_computation.1 | async-start | bytes 2097152 | tf_op jit(solution)/shard_map/all_to_all | solution.py:110
  92.6 0.1 add_cosine_fusion
  92.8 0.8 slice_bitcast_fusion.1
  93.6 18.0 %all-to-all-done.1 = f32[128,8,256]{2,1,0:T(8,128)S(1)} async-done(((f32[128,8,256]{2,1,0:T(8,128)}), f32[128,8,256]{2,1,0:T(8,128)S(1)}, u32[]{:S(2)}, u32[]{:S(2)}) %all-to-all-start.1) | async-done | bytes 1048608 | tf_op jit(solution)/shard_map/all_to_all | solution.py:110
  111.5 0.3 copy.109
  111.9 2.2 %fusion.1 = f32[1024,4,64]{0,2,1:T(8,128)S(1)} fusion(f32[4,64,1024]{2,1,0:T(8,128)S(1)} %bitcast.153, s32[1024]{0:T(1024)S(1)} %bitcast.171), kind=kOutput, calls=%fused_computation.3 | convolution fusion | flops 3222274048 | bytes 2101248 | tf_op jit(solution)/shard_map/kp,pm->km/dot_general | solution.py:18
  114.1 0.2 multiply_add_fusion
  114.3 2.0 multiply_reduce_fusion.8
  116.4 0.7 reshape.236
  117.1 3.5 %all-to-all-start.2 = ((f32[16,1,512]{2,1,0:T(1,128)}), f32[16,1,512]{2,1,0:T(1,128)S(1)}, u32[]{:S(2)}, u32[]{:S(2)}) async-start(f32[16,1,512]{2,1,0:T(1,128)} %reshape.236), calls=%async_computation.2 | async-start | bytes 65536 | tf_op jit(solution)/shard_map/all_to_all | solution.py:127
  120.6 7.6 %all-to-all-done.2 = f32[16,1,512]{2,1,0:T(1,128)S(1)} async-done(((f32[16,1,512]{2,1,0:T(1,128)}), f32[16,1,512]{2,1,0:T(1,128)S(1)}, u32[]{:S(2)}, u32[]{:S(2)}) %all-to-all-start.2) | async-done | bytes 32800 | tf_op jit(solution)/shard_map/all_to_all | solution.py:127
  128.1 0.5 broadcast.176
  128.6 0.6 reduce.4
  129.3 0.1 reshape.237
  129.5 59.8 %all-gather.5.cloned.1.call-done = f32[2,4096,256]{1,2,0:T(8,128)} async-done(((f32[2,256,256]{1,2,0:T(8,128)}), f32[2,4096,256]{1,2,0:T(8,128)}) %all-gather.5.cloned.1.call-update) | async-done | bytes 8388624 | tf_op jit(solution)/shard_map/all_gather | solution.py:129
  189.3 13.3 %fusion.51 = f32[2,256,256]{2,1,0:T(8,128)S(1)} fusion(f32[2,4096,256]{1,2,0:T(8,128)} %all-gather.5.cloned.1.call-done, f32[2,256,4096]{2,1,0:T(8,128)} %param.14), kind=kOutput, calls=%fused_computation.91 | convolution fusion | flops 3221225472 | bytes 17301504 | tf_op jit(solution)/shard_map/srj,sjm->srm/dot_general | solution.py:22
  202.6 0.1 multiply_subtract_fusion
  202.7 0.1 maximum_bitcast_fusion.2
  202.8 1.1 copy.111
  (65 shorter events, 1.2 us)
Async XLA Ops:
  6.5 62.4 %all-gather.3.cloned.1.call-start = ((), (), s32[]{:S(2)}) async-start(), calls=%async_computation.3 | async-start | bytes 4456448 | tf_op jit(solution)/shard_map/all_gather | solution.py:52
  8.9 14.0 %slice-start = ((s8[8388608]{0:T(1024)(128)(4,1)}), s8[4194304]{0:T(1024)(128)(4,1)S(1)}, s32[]{:S(2)}) async-start(s8[8388608]{0:T(1024)(128)(4,1)} %bitcast.138), calls=%async_computation.5 | async-start | bytes 8388608
  9.0 13.2 %copy-start.10 = (s32[1024]{0:T(1024)S(1)}, s32[1024]{0:T(1024)}, u32[]{:S(2)}) copy-start(s32[1024]{0:T(1024)} %param.20) | copy-start | bytes 12292
  9.0 14.0 %slice-start.1 = ((s8[8388608]{0:T(1024)(128)(4,1)}), s8[4194304]{0:T(1024)(128)(4,1)S(1)}, s32[]{:S(2)}) async-start(s8[8388608]{0:T(1024)(128)(4,1)} %bitcast.138), calls=%async_computation.6 | async-start | bytes 8388608
  9.0 14.0 %copy-start.7 = (s32[2,64]{1,0:T(2,128)S(1)}, s32[2,64]{1,0:T(2,128)}, u32[]{:S(2)}) copy-start(s32[2,64]{1,0:T(2,128)} %param.22) | copy-start | bytes 1540
  23.0 14.1 %copy-start.2 = (f32[4]{0:T(128)S(1)}, f32[4]{0:T(128)}, u32[]{:S(2)}) copy-start(f32[4]{0:T(128)} %constant.24.clone) | copy-start | bytes 52
  23.0 14.2 %copy-start.3 = (f32[4]{0:T(128)S(1)}, f32[4]{0:T(128)}, u32[]{:S(2)}) copy-start(f32[4]{0:T(128)} %constant.25.clone) | copy-start | bytes 52
  23.1 14.9 %copy-start.5 = (s32[1,1024]{1,0:T(1,128)S(1)}, s32[1,1024]{1,0:T(1,128)}, u32[]{:S(2)}) copy-start(s32[1,1024]{1,0:T(1,128)} %param.21) | copy-start | bytes 12292
  23.1 16.3 %copy-start.4 = (f32[1024]{0:T(1024)S(1)}, f32[1024]{0:T(1024)}, u32[]{:S(2)}) copy-start(f32[1024]{0:T(1024)} %param.19) | copy-start | bytes 12292
  28.9 16.2 %all-to-all-start = ((f32[16,2,6,256]{3,1,2,0:T(2,128)}), f32[16,2,6,256]{3,1,2,0:T(2,128)S(1)}, u32[]{:S(2)}, u32[]{:S(2)}) async-start(f32[16,2,6,256]{3,1,2,0:T(2,128)} %broadcast_in_dim.17), calls=%async_computation | async-start | bytes 393216 | tf_op jit(solution)/shard_map/all_to_all | solution.py:82
  45.3 7.0 %copy-start.8 = (f32[2,64]{1,0:T(2,128)S(1)}, f32[2,64]{1,0:T(2,128)}, u32[]{:S(2)}) copy-start(f32[2,64]{1,0:T(2,128)} %param.24) | copy-start | bytes 1540
  45.3 7.1 %copy-start.6 = (s32[2,64]{1,0:T(2,128)S(1)}, s32[2,64]{1,0:T(2,128)}, u32[]{:S(2)}) copy-start(s32[2,64]{1,0:T(2,128)} %param.23) | copy-start | bytes 1540
  84.6 8.0 %copy-start.1 = (f32[2,256]{1,0:T(2,128)S(1)}, f32[2,256]{1,0:T(2,128)}, u32[]{:S(2)}) copy-start(f32[2,256]{1,0:T(2,128)} %param.16) | copy-start | bytes 6148
  84.6 8.1 %copy-start.9 = (f32[4]{0:T(128)S(1)}, f32[4]{0:T(128)}, u32[]{:S(2)}) copy-start(f32[4]{0:T(128)} %constant.26.clone) | copy-start | bytes 52
  84.6 27.0 %all-to-all-start.1 = ((f32[128,8,256]{2,1,0:T(8,128)}), f32[128,8,256]{2,1,0:T(8,128)S(1)}, u32[]{:S(2)}, u32[]{:S(2)}) async-start(f32[128,8,256]{2,1,0:T(8,128)} %fusion.4), calls=%async_computation.1 | async-start | bytes 2097152 | tf_op jit(solution)/shard_map/all_to_all | solution.py:110
  92.5 96.8 %all-gather.5.cloned.1.call-start = ((), (), s32[]{:S(2)}) async-start(), calls=%async_computation.4 | async-start | bytes 8912896 | tf_op jit(solution)/shard_map/all_gather | solution.py:129
  111.9 2.4 %copy-start = (f32[2,64,256]{2,1,0:T(8,128)S(1)}, f32[2,64,256]{2,1,0:T(8,128)}, u32[]{:S(2)}) copy-start(f32[2,64,256]{2,1,0:T(8,128)} %param.15) | copy-start | bytes 393220
  117.1 11.1 %all-to-all-start.2 = ((f32[16,1,512]{2,1,0:T(1,128)}), f32[16,1,512]{2,1,0:T(1,128)S(1)}, u32[]{:S(2)}, u32[]{:S(2)}) async-start(f32[16,1,512]{2,1,0:T(1,128)} %reshape.236), calls=%async_computation.2 | async-start | bytes 65536 | tf_op jit(solution)/shard_map/all_to_all | solution.py:127
Sparse Core Ops, SparseCore 0:
  9.4 59.4 all-gather.2
  116.5 72.7 all-gather.4

commit v3 on v2

--- a/solution.py
+++ b/solution.py
@@ -46,10 +46,10 @@
     row_ids = lax.axis_index("node") * rows + lax.iota(jnp.int32, rows)
 
     amp_t = jnp.transpose(source_amp, (0, 2, 1))
+    packed = lax.optimization_barrier(amp_t.reshape(subnets, rows // 2, 2 * cases))
+    amp_full = lax.all_gather(packed, "node", axis=1, tiled=True).reshape(subnets, order, cases)
     amp_cos = amp_t * jnp.cos(source_angle)[:, :, None]
     amp_sin = amp_t * jnp.sin(source_angle)[:, :, None]
-    amp_cos, amp_sin = lax.optimization_barrier((amp_cos, amp_sin))
-    sources = lax.all_gather(jnp.concatenate([amp_cos, amp_sin], axis=2), "node", axis=1, tiled=True)
 
     local_ids = lax.iota(jnp.int32, local)
     attach_map = (attach[:, None] == local_ids[None, :]).astype(jnp.float32)
@@ -77,11 +77,18 @@
     ).reshape(subnets, -1)
     pad_len = 2 * rows - partials.shape[1]
     partials = jnp.concatenate([partials, jnp.zeros((subnets, pad_len), jnp.float32)], axis=1)
-    small = jnp.concatenate([h0, partials.reshape(subnets, 2, rows)], axis=1)
+    small = jnp.concatenate(
+        [h0, partials.reshape(subnets, 2, rows), source_angle[:, None], jnp.zeros((subnets, 1, rows), jnp.float32)],
+        axis=1,
+    )
     small = jnp.broadcast_to(small[None], (n_node,) + small.shape)
     small = lax.all_to_all(small, "node", 0, 0, tiled=True)
     h0_full = jnp.transpose(small[:, :, :steps], (1, 0, 3, 2)).reshape(subnets, order, steps)
-    sums = jnp.sum(small[:, :, steps:], axis=0).reshape(subnets, 2 * rows)
+    sums = jnp.sum(small[:, :, steps : steps + 2], axis=0).reshape(subnets, 2 * rows)
+    angle_full = jnp.transpose(small[:, :, steps + 2], (1, 0, 2)).reshape(subnets, order)
+    sources = jnp.concatenate(
+        [amp_full * jnp.cos(angle_full)[:, :, None], amp_full * jnp.sin(angle_full)[:, :, None]], axis=2
+    )
     sums = sums[:, : 7 * cases].reshape(subnets, 7, cases)
     denominator = sums[:, 6] + fault_res
 

time: 211 us -> 206 us (0.976)
  waiting for transfers between devices: 108 us -> 93.3 us
  local copies, waits for them, and re-layouts: 7.5 us -> 17.7 us
    all_gather x1, waiting for transfers between devices: 16.5 us -> 2.91 us  [body(): lax.all_gather(packed, 'node', axis=1, tiled=True)]
    reshape x1 -> x4, local copies, waits for them, and re-layouts: 0.02 us -> 8.16 us  [the longest x2 7.38 us: body(): lax.all_gather(packed, 'node', axis=1, tiled=True)]
  transfers between devices with their start and end apart: 5 -> 5, of which waited for: 5 -> 5; matrix products, arithmetic and copies ran while one was open for 15% -> 17% of each run, Pallas kernels for 0% -> 0%
where the time goes in v3:
time: 206 us; the launch traced here: 205 us
  waiting for transfers between devices  93.3 us (45%)
  matrix products  55.9 us (27%)
  starting transfers between devices  19.7 us (10%)
  local copies, waits for them, and re-layouts  17.7 us (9%)
  between operations  14 us (7%)
  other arithmetic  4.7 us (2%)
    all_gather x1, waiting for transfers between devices, body(): lax.all_gather(inj1.reshape(subnets, rows, steps * cases), 'node', axis=1...  59.8 us
    dot_general x8, matrix products, mm(): jnp.einsum(spec, a, b, precision=PRECISE, preferred_element_type=jnp.floa...  28.1 us
    dot_general x3, matrix products, fast(): jnp.einsum(spec, a, b, precision=lax.Precision.HIGH, preferred_element_ty...  27.8 us
    all_to_all x1, waiting for transfers between devices, body(): incoming = lax.all_to_all(outgoing, ('region', 'node'), 0, 0, tiled=True)  17.7 us
    all_to_all x1, starting transfers between devices, body(): small = lax.all_to_all(small, 'node', 0, 0, tiled=True)  8 us
    all_to_all x1, starting transfers between devices, body(): incoming = lax.all_to_all(outgoing, ('region', 'node'), 0, 0, tiled=True)  7.94 us
    all_to_all x1, waiting for transfers between devices, body(): lax.all_to_all(jnp.broadcast_to(part1[None], (n_node,) + part1.shape), 'n...  7.56 us
    reshape x2, local copies, waits for them, and re-layouts, body(): lax.all_gather(packed, 'node', axis=1, tiled=True)  7.38 us
  transfers between devices with their start and end apart: 5, of which 5 were waited for; matrix products, arithmetic and copies ran while one was open for 17% of the time, Pallas kernels for 0%

profile of v3, /device:TPU:0, one launch (start us, length us, event | category | flops | bytes accessed | tf_op | source)
XLA Modules:
  0.0 205.2 jit_solution(8276969634973273132)
XLA Ops:
  6.5 1.0 copy.78
  7.6 0.8 reshape.233
  8.4 0.7 fusion.57
  9.2 13.2 %multiply_reduce_fusion.3 = (f32[1024]{0:T(1024)S(1)}, f32[1024]{0:T(1024)S(1)}, f32[1024]{0:T(1024)S(1)}, f32[1024]{0:T(1024)S(1)}, f32[1024]{0:T(1024)S(1)}, /...) fusion(f32[515,1024]{1,0:T(8,128)} %param.18, f32[512,1024]{1,0:T(8,128)} %param.17), kind=kOutput, calls=%fused_computation.15 | convolution fusion | flops 3230130176 | bytes 12648448 | tf_op jit(solution)/shard_map/uj,jk->uk/dot_general | solution.py:18
  22.3 0.8 fusion.12
  23.2 4.7 %multiply_reduce_fusion.10 = (f32[2,64]{1,0:T(2,128)S(1)}, f32[2,64]{1,0:T(2,128)S(1)}, f32[2,64]{1,0:T(2,128)S(1)}, f32[2,64,256]{2,1,0:T(8,128)S(1)}) fusion(f32[2,256]{1,0:T(2,128)S(1)} %get-tuple-element.40, f32[2,64,256]{2,1,0:T(8,128)S(1)} %copy-done.1, f32[2,256]{1,0:T(2,128)S(1)} %get-tuple-element.39, s32[2,64]{1,0:T(2,128)S(1)} %copy-done.9, ...), kind=kOutput, calls=%fused_computation.68 | convolution fusion | flops 1611431552 | bytes 8657920 | tf_op jit(solution)/shard_map/srj,sjc->src/dot_general | solution.py:18
  28.0 0.2 fusion.58
  28.5 0.7 broadcast_in_dim.23
  29.2 8.0 %all-to-all-start = ((f32[16,2,8,256]{3,2,1,0:T(8,128)}), f32[16,2,8,256]{3,2,1,0:T(8,128)S(1)}, u32[]{:S(2)}, u32[]{:S(2)}) async-start(f32[16,2,8,256]{3,2,1,0:T(8,128)} %broadcast_in_dim.23), calls=%async_computation | async-start | bytes 524288 | tf_op jit(solution)/shard_map/all_to_all | solution.py:85
  37.2 0.5 broadcast.177
  37.7 0.7 reduce.3
  38.5 1.6 fusion.7
  40.5 5.2 %all-to-all-done = f32[16,2,8,256]{3,2,1,0:T(8,128)S(1)} async-done(((f32[16,2,8,256]{3,2,1,0:T(8,128)}), f32[16,2,8,256]{3,2,1,0:T(8,128)S(1)}, u32[]{:S(2)}, u32[]{:S(2)}) %all-to-all-start) | async-done | bytes 262176 | tf_op jit(solution)/shard_map/all_to_all | solution.py:85
  45.7 1.0 slice_cosine_fusion
  47.0 6.9 %convolution_bitcast_fusion = f32[2,256,4]{1,2,0:T(4,128)S(1)} fusion(f32[2,4096,4]{1,2,0:T(4,128)S(1)} %bitcast.166, f32[2,256,4096]{2,1,0:T(8,128)} %param.14), kind=kOutput, calls=%fused_computation.33 | convolution fusion | flops 50331648 | bytes 8527872 | tf_op jit(solution)/shard_map/srj,sjt->srt/dot_general | solution.py:22
  53.9 0.1 add.142.clone
  54.2 2.9 %all-gather.3.cloned.1.call-done = f32[2,2048,128]{2,1,0:T(8,128)} async-done(((f32[2,128,128]{2,1,0:T(8,128)}), f32[2,2048,128]{2,1,0:T(8,128)}) %all-gather.3.cloned.1.call-update) | async-done | bytes 2097168 | tf_op jit(solution)/shard_map/all_gather | solution.py:50
  57.1 4.3 %reshape.234 = f32[2,4096,64]{2,1,0:T(8,128)} reshape(f32[2,2048,128]{2,1,0:T(8,128)} %all-gather.3.cloned.1.call-done) | data formatting | bytes 4194304 | tf_op jit(solution)/shard_map/reshape | solution.py:50
  61.4 3.0 %copy.84 = f32[2,4096,64]{1,2,0:T(8,128)S(1)} copy(f32[2,4096,64]{2,1,0:T(8,128)} %reshape.234) | data formatting | bytes 4194304 | tf_op jit(solution)/shard_map/reshape | solution.py:50
  64.5 0.5 broadcast_multiply_fusion.1
  65.0 7.6 %fusion.28 = f32[2,256,128]{1,2,0:T(8,128)S(1)} fusion(f32[2,256,4096]{2,1,0:T(8,128)} %param.14, f32[2,4096,64]{1,2,0:T(8,128)S(1)} %get-tuple-element.17, f32[2,4096,64]{1,2,0:T(8,128)S(1)} %get-tuple-element.16), kind=kOutput, calls=%fused_computation.32 | convolution fusion | flops 1611661312 | bytes 12845056 | tf_op jit(solution)/shard_map/srj,sjc->src/dot_general | solution.py:22
  72.6 0.1 copy.105
  72.7 0.1 copy.106
  72.9 0.2 add_subtract_fusion.1
  73.0 0.4 copy.91
  73.5 0.1 mul.303.clone
  73.7 0.1 mul.306.clone
  73.9 0.2 add_subtract_fusion
  74.1 1.2 fusion.22
  75.3 3.7 %fusion.8 = f32[128,8,256]{2,1,0:T(8,128)} fusion(f32[1024,256,1]{0,1,2:T(8,128)S(1)} %bitcast.203, pred[128,8,1024]{2,0,1:T(32,128)(4,1)S(1)} %copy-done), kind=kOutput, calls=%fused_computation.9 | convolution fusion | flops 3221225472 | bytes 3145728 | tf_op jit(solution)/shard_map/pk,km->pm/dot_general | solution.py:18
  79.0 7.9 %all-to-all-start.1 = ((f32[128,8,256]{2,1,0:T(8,128)}), f32[128,8,256]{2,1,0:T(8,128)S(1)}, u32[]{:S(2)}, u32[]{:S(2)}) async-start(f32[128,8,256]{2,1,0:T(8,128)} %fusion.8), calls=%async_computation.1 | async-start | bytes 2097152 | tf_op jit(solution)/shard_map/all_to_all | solution.py:117
  87.0 0.3 all-gather.5.cloned.1.call-start
  87.4 0.1 add_cosine_fusion
  87.5 0.8 slice_bitcast_fusion.1
  88.3 17.7 %all-to-all-done.1 = f32[128,8,256]{2,1,0:T(8,128)S(1)} async-done(((f32[128,8,256]{2,1,0:T(8,128)}), f32[128,8,256]{2,1,0:T(8,128)S(1)}, u32[]{:S(2)}, u32[]{:S(2)}) %all-to-all-start.1) | async-done | bytes 1048608 | tf_op jit(solution)/shard_map/all_to_all | solution.py:117
  106.0 0.3 copy.94
  106.4 2.2 %fusion.5 = f32[1024,4,64]{0,2,1:T(8,128)S(1)} fusion(f32[4,64,1024]{2,1,0:T(8,128)S(1)} %bitcast.163, s32[1024]{0:T(1024)S(1)} %bitcast.184), kind=kOutput, calls=%fused_computation.7 | convolution fusion | flops 3222274048 | bytes 2101248 | tf_op jit(solution)/shard_map/kp,pm->km/dot_general | solution.py:18
  108.5 0.2 multiply_add_fusion
  108.7 2.0 multiply_reduce_fusion.8
  110.8 0.7 reshape.260
  111.5 3.5 %all-to-all-start.2 = ((f32[16,1,512]{2,1,0:T(1,128)}), f32[16,1,512]{2,1,0:T(1,128)S(1)}, u32[]{:S(2)}, u32[]{:S(2)}) async-start(f32[16,1,512]{2,1,0:T(1,128)} %reshape.260), calls=%async_computation.2 | async-start | bytes 65536 | tf_op jit(solution)/shard_map/all_to_all | solution.py:134
  115.0 7.6 %all-to-all-done.2 = f32[16,1,512]{2,1,0:T(1,128)S(1)} async-done(((f32[16,1,512]{2,1,0:T(1,128)}), f32[16,1,512]{2,1,0:T(1,128)S(1)}, u32[]{:S(2)}, u32[]{:S(2)}) %all-to-all-start.2) | async-done | bytes 32800 | tf_op jit(solution)/shard_map/all_to_all | solution.py:134
  122.6 0.5 broadcast.178
  123.1 0.6 reduce.4
  123.9 59.8 %all-gather.5.cloned.1.call-done = f32[2,4096,256]{1,2,0:T(8,128)} async-done(((f32[2,256,256]{1,2,0:T(8,128)}), f32[2,4096,256]{1,2,0:T(8,128)}) %all-gather.5.cloned.1.call-update) | async-done | bytes 8388624 | tf_op jit(solution)/shard_map/all_gather | solution.py:136
  183.8 13.3 %fusion.59 = f32[2,256,256]{2,1,0:T(8,128)S(1)} fusion(f32[2,4096,256]{1,2,0:T(8,128)} %all-gather.5.cloned.1.call-done, f32[2,256,4096]{2,1,0:T(8,128)} %param.14), kind=kOutput, calls=%fused_computation.97 | convolution fusion | flops 3221225472 | bytes 17301504 | tf_op jit(solution)/shard_map/srj,sjm->srm/dot_general | solution.py:22
  197.1 0.1 multiply_subtract_fusion
  197.3 1.1 copy.96
  (74 shorter events, 1.7 us)
Async XLA Ops:
  6.5 50.6 %all-gather.3.cloned.1.call-start = ((), (), s32[]{:S(2)}) async-start(), calls=%async_computation.3 | async-start | bytes 2228224 | tf_op jit(solution)/shard_map/all_gather | solution.py:50
  9.1 14.1 %slice-start = ((s8[8388608]{0:T(1024)(128)(4,1)}), s8[4194304]{0:T(1024)(128)(4,1)S(1)}, s32[]{:S(2)}) async-start(s8[8388608]{0:T(1024)(128)(4,1)} %bitcast.148), calls=%async_computation.5 | async-start | bytes 8388608
  9.1 13.2 %copy-start.11 = (s32[1024]{0:T(1024)S(1)}, s32[1024]{0:T(1024)}, u32[]{:S(2)}) copy-start(s32[1024]{0:T(1024)} %param.20) | copy-start | bytes 12292
  9.1 14.0 %slice-start.1 = ((s8[8388608]{0:T(1024)(128)(4,1)}), s8[4194304]{0:T(1024)(128)(4,1)S(1)}, s32[]{:S(2)}) async-start(s8[8388608]{0:T(1024)(128)(4,1)} %bitcast.148), calls=%async_computation.6 | async-start | bytes 8388608
  9.2 14.0 %copy-start.1 = (f32[2,64,256]{2,1,0:T(8,128)S(1)}, f32[2,64,256]{2,1,0:T(8,128)}, u32[]{:S(2)}) copy-start(f32[2,64,256]{2,1,0:T(8,128)} %param.15) | copy-start | bytes 393220
  9.2 14.0 %copy-start.9 = (s32[2,64]{1,0:T(2,128)S(1)}, s32[2,64]{1,0:T(2,128)}, u32[]{:S(2)}) copy-start(s32[2,64]{1,0:T(2,128)} %param.22) | copy-start | bytes 1540
  23.2 5.1 %copy-start.2 = (f32[2,256]{1,0:T(2,128)S(1)}, f32[2,256]{1,0:T(2,128)}, u32[]{:S(2)}) copy-start(f32[2,256]{1,0:T(2,128)} %param.16) | copy-start | bytes 6148
  23.2 14.5 %copy-start.6 = (s32[1,1024]{1,0:T(1,128)S(1)}, s32[1,1024]{1,0:T(1,128)}, u32[]{:S(2)}) copy-start(s32[1,1024]{1,0:T(1,128)} %param.21) | copy-start | bytes 12292
  28.0 12.3 %copy-start.3 = (f32[4]{0:T(128)S(1)}, f32[4]{0:T(128)}, u32[]{:S(2)}) copy-start(f32[4]{0:T(128)} %constant.8.clone) | copy-start | bytes 52
  28.0 12.4 %copy-start.4 = (f32[4]{0:T(128)S(1)}, f32[4]{0:T(128)}, u32[]{:S(2)}) copy-start(f32[4]{0:T(128)} %constant.26.clone) | copy-start | bytes 52
  28.0 12.6 %copy-start.5 = (f32[1024]{0:T(1024)S(1)}, f32[1024]{0:T(1024)}, u32[]{:S(2)}) copy-start(f32[1024]{0:T(1024)} %param.19) | copy-start | bytes 12292
  29.2 16.5 %all-to-all-start = ((f32[16,2,8,256]{3,2,1,0:T(8,128)}), f32[16,2,8,256]{3,2,1,0:T(8,128)S(1)}, u32[]{:S(2)}, u32[]{:S(2)}) async-start(f32[16,2,8,256]{3,2,1,0:T(8,128)} %broadcast_in_dim.23), calls=%async_computation | async-start | bytes 524288 | tf_op jit(solution)/shard_map/all_to_all | solution.py:85
  46.9 7.1 %copy-start.8 = (f32[2,64]{1,0:T(2,128)S(1)}, f32[2,64]{1,0:T(2,128)}, u32[]{:S(2)}) copy-start(f32[2,64]{1,0:T(2,128)} %param.24) | copy-start | bytes 1540
  47.0 7.2 %copy-start.7 = (s32[2,64]{1,0:T(2,128)S(1)}, s32[2,64]{1,0:T(2,128)}, u32[]{:S(2)}) copy-start(s32[2,64]{1,0:T(2,128)} %param.23) | copy-start | bytes 1540
  73.9 1.4 copy-start
  79.0 8.3 %copy-start.10 = (f32[4]{0:T(128)S(1)}, f32[4]{0:T(128)}, u32[]{:S(2)}) copy-start(f32[4]{0:T(128)} %constant.27.clone) | copy-start | bytes 52
  79.0 27.0 %all-to-all-start.1 = ((f32[128,8,256]{2,1,0:T(8,128)}), f32[128,8,256]{2,1,0:T(8,128)S(1)}, u32[]{:S(2)}, u32[]{:S(2)}) async-start(f32[128,8,256]{2,1,0:T(8,128)} %fusion.8), calls=%async_computation.1 | async-start | bytes 2097152 | tf_op jit(solution)/shard_map/all_to_all | solution.py:117
  87.0 96.8 %all-gather.5.cloned.1.call-start = ((), (), s32[]{:S(2)}) async-start(), calls=%async_computation.4 | async-start | bytes 8912896 | tf_op jit(solution)/shard_map/all_gather | solution.py:136
  111.5 11.1 %all-to-all-start.2 = ((f32[16,1,512]{2,1,0:T(1,128)}), f32[16,1,512]{2,1,0:T(1,128)S(1)}, u32[]{:S(2)}, u32[]{:S(2)}) async-start(f32[16,1,512]{2,1,0:T(1,128)} %reshape.260), calls=%async_computation.2 | async-start | bytes 65536 | tf_op jit(solution)/shard_map/all_to_all | solution.py:134
Sparse Core Ops, SparseCore 0:
  9.5 47.5 all-gather.2
  110.9 72.7 all-gather.4

commit v4 on v3

--- a/solution.py
+++ b/solution.py
@@ -46,8 +46,7 @@
     row_ids = lax.axis_index("node") * rows + lax.iota(jnp.int32, rows)
 
     amp_t = jnp.transpose(source_amp, (0, 2, 1))
-    packed = lax.optimization_barrier(amp_t.reshape(subnets, rows // 2, 2 * cases))
-    amp_full = lax.all_gather(packed, "node", axis=1, tiled=True).reshape(subnets, order, cases)
+    amp_full = lax.all_gather(lax.optimization_barrier(source_amp), "node", axis=2, tiled=True)
     amp_cos = amp_t * jnp.cos(source_angle)[:, :, None]
     amp_sin = amp_t * jnp.sin(source_angle)[:, :, None]
 
@@ -87,12 +86,12 @@
     sums = jnp.sum(small[:, :, steps : steps + 2], axis=0).reshape(subnets, 2 * rows)
     angle_full = jnp.transpose(small[:, :, steps + 2], (1, 0, 2)).reshape(subnets, order)
     sources = jnp.concatenate(
-        [amp_full * jnp.cos(angle_full)[:, :, None], amp_full * jnp.sin(angle_full)[:, :, None]], axis=2
+        [amp_full * jnp.cos(angle_full)[:, None, :], amp_full * jnp.sin(angle_full)[:, None, :]], axis=1
     )
     sums = sums[:, : 7 * cases].reshape(subnets, 7, cases)
     denominator = sums[:, 6] + fault_res
 
-    prod = fast("srj,sjc->src", impedance, sources)
+    prod = fast("srj,scj->src", impedance, sources)
     prod_h = fast("srj,sjt->srt", impedance, h0_full)
     t0 = lax.iota(jnp.int32, steps)
     cw = jnp.asarray(np.cos(omega_step * np.arange(steps)), jnp.float32)

time: 206 us -> 202 us (0.981)
  local copies, waits for them, and re-layouts: 17.7 us -> 8.69 us
  waiting for transfers between devices: 93.3 us -> 98.3 us
    reshape x3 -> x0, local copies, waits for them, and re-layouts: 8.14 us -> none  [the longest x2 7.38 us: body(): lax.all_gather(packed, 'node', axis=1, tiled=True)]
    all_gather x1, waiting for transfers between devices: 2.91 us -> 5.98 us  [body(): lax.all_gather(lax.optimization_barrier(source_amp), 'node', axis=2, tile...]
where the time goes in v4:
time: 202 us
  waiting for transfers between devices  98.3 us (49%)
  matrix products  55.8 us (28%)
  starting transfers between devices  19.4 us (10%)
  between operations  13.9 us (7%)
  local copies, waits for them, and re-layouts  8.69 us (4%)
  other arithmetic  5.41 us (3%)
    all_gather x1, waiting for transfers between devices, body(): lax.all_gather(inj1.reshape(subnets, rows, steps * cases), 'node', axis=1...  59.8 us
    dot_general x8, matrix products, mm(): jnp.einsum(spec, a, b, precision=PRECISE, preferred_element_type=jnp.floa...  28.1 us
    dot_general x3, matrix products, fast(): jnp.einsum(spec, a, b, precision=lax.Precision.HIGH, preferred_element_ty...  27.7 us
    all_to_all x1, waiting for transfers between devices, body(): incoming = lax.all_to_all(outgoing, ('region', 'node'), 0, 0, tiled=True)  18 us
    all_to_all x1, starting transfers between devices, body(): small = lax.all_to_all(small, 'node', 0, 0, tiled=True)  7.99 us
    all_to_all x1, starting transfers between devices, body(): incoming = lax.all_to_all(outgoing, ('region', 'node'), 0, 0, tiled=True)  7.93 us
    all_to_all x1, waiting for transfers between devices, body(): lax.all_to_all(jnp.broadcast_to(part1[None], (n_node,) + part1.shape), 'n...  7.56 us
    all_to_all x1, waiting for transfers between devices, body(): small = lax.all_to_all(small, 'node', 0, 0, tiled=True)  6.18 us
  transfers between devices with their start and end apart: 5, of which 5 were waited for; matrix products, arithmetic and copies ran while one was open for 17% of the time, Pallas kernels for 0%

profile of v4, /device:TPU:0, one launch (start us, length us, event | category | flops | bytes accessed | tf_op | source)
XLA Modules:
  0.0 201.5 jit_solution(13758653417945175726)
XLA Ops:
  6.5 0.7 all-gather.3.cloned.1.call-update
  7.3 0.7 fusion.57
  8.1 13.1 %multiply_reduce_fusion.3 = (f32[1024]{0:T(1024)S(1)}, f32[1024]{0:T(1024)S(1)}, f32[1024]{0:T(1024)S(1)}, f32[1024]{0:T(1024)S(1)}, f32[1024]{0:T(1024)S(1)}, /...) fusion(f32[515,1024]{1,0:T(8,128)} %param.18, f32[512,1024]{1,0:T(8,128)} %param.17), kind=kOutput, calls=%fused_computation.15 | convolution fusion | flops 3230130176 | bytes 12648448 | tf_op jit(solution)/shard_map/uj,jk->uk/dot_general | solution.py:18
  21.2 0.8 fusion.12
  22.1 4.7 %multiply_reduce_fusion.10 = (f32[2,64]{1,0:T(2,128)S(1)}, f32[2,64]{1,0:T(2,128)S(1)}, f32[2,64]{1,0:T(2,128)S(1)}, f32[2,64,256]{2,1,0:T(8,128)S(1)}) fusion(f32[2,256]{1,0:T(2,128)S(1)} %get-tuple-element.40, f32[2,64,256]{2,1,0:T(8,128)S(1)} %copy-done, f32[2,256]{1,0:T(2,128)S(1)} %get-tuple-element.39, s32[2,64]{1,0:T(2,128)S(1)} %copy-done.8, ...), kind=kOutput, calls=%fused_computation.68 | convolution fusion | flops 1611431552 | bytes 8657920 | tf_op jit(solution)/shard_map/srj,sjc->src/dot_general | solution.py:18
  26.9 0.2 fusion.58
  27.4 0.7 broadcast_in_dim.23
  28.1 8.0 %all-to-all-start = ((f32[16,2,8,256]{3,2,1,0:T(8,128)}), f32[16,2,8,256]{3,2,1,0:T(8,128)S(1)}, u32[]{:S(2)}, u32[]{:S(2)}) async-start(f32[16,2,8,256]{3,2,1,0:T(8,128)} %broadcast_in_dim.23), calls=%async_computation | async-start | bytes 524288 | tf_op jit(solution)/shard_map/all_to_all | solution.py:84
  36.1 0.5 broadcast.177
  36.6 0.6 reduce.3
  37.3 0.1 eq.136
  37.4 0.7 fusion.7
  38.2 0.1 mul.331
  38.5 6.2 %all-to-all-done = f32[16,2,8,256]{3,2,1,0:T(8,128)S(1)} async-done(((f32[16,2,8,256]{3,2,1,0:T(8,128)}), f32[16,2,8,256]{3,2,1,0:T(8,128)S(1)}, u32[]{:S(2)}, u32[]{:S(2)}) %all-to-all-start) | async-done | bytes 262176 | tf_op jit(solution)/shard_map/all_to_all | solution.py:84
  44.6 1.1 slice_cosine_fusion
  46.0 6.7 %convolution_bitcast_fusion = f32[2,256,4]{1,2,0:T(4,128)S(1)} fusion(f32[2,4096,4]{1,2,0:T(4,128)S(1)} %bitcast.165, f32[2,256,4096]{2,1,0:T(8,128)} %param.14), kind=kOutput, calls=%fused_computation.33 | convolution fusion | flops 50331648 | bytes 8527872 | tf_op jit(solution)/shard_map/srj,sjt->srt/dot_general | solution.py:22
  52.8 0.1 add.142.clone
  53.1 6.0 %all-gather.3.cloned.1.call-done = f32[2,64,4096]{2,1,0:T(8,128)} async-done(((f32[2,64,256]{2,1,0:T(8,128)}), f32[2,64,4096]{2,1,0:T(8,128)}) %all-gather.3.cloned.1.call-update) | async-done | bytes 2097168 | tf_op jit(solution)/shard_map/all_gather | solution.py:49
  59.1 2.1 %broadcast_multiply_fusion.1 = (f32[2,64,4096]{2,1,0:T(8,128)S(1)}, f32[2,64,4096]{2,1,0:T(8,128)S(1)}) fusion(f32[2,64,4096]{2,1,0:T(8,128)} %all-gather.3.cloned.1.call-done, f32[2,4096]{1,0:T(2,128)S(1)} %bitcast.168, f32[2,4096]{1,0:T(2,128)S(1)} %bitcast.169), kind=kLoop, calls=%fused_computation.45 | loop fusion | flops 1048576 | bytes 6356992 | tf_op jit(solution)/shard_map/mul | solution.py:89
  61.3 7.6 %fusion.28 = f32[2,256,128]{1,2,0:T(8,128)S(1)} fusion(f32[2,256,4096]{2,1,0:T(8,128)} %param.14, f32[2,64,4096]{2,1,0:T(8,128)S(1)} %get-tuple-element.17, f32[2,64,4096]{2,1,0:T(8,128)S(1)} %get-tuple-element.16), kind=kOutput, calls=%fused_computation.32 | convolution fusion | flops 1611661312 | bytes 12845056 | tf_op jit(solution)/shard_map/srj,scj->src/dot_general | solution.py:22
  68.9 0.1 copy.93
  69.0 0.1 copy.94
  69.2 0.2 add_subtract_fusion.1
  69.3 0.4 copy.79
  69.8 0.1 mul.303.clone
  70.0 0.1 mul.306.clone
  70.2 0.2 add_subtract_fusion
  70.4 1.3 fusion.22
  71.6 3.7 %fusion.8 = f32[128,8,256]{2,1,0:T(8,128)} fusion(f32[1024,256,1]{0,1,2:T(8,128)S(1)} %bitcast.202, pred[128,8,1024]{2,0,1:T(32,128)(4,1)S(1)} %fusion.7), kind=kOutput, calls=%fused_computation.9 | convolution fusion | flops 3221225472 | bytes 3145728 | tf_op jit(solution)/shard_map/pk,km->pm/dot_general | solution.py:18
  75.4 7.9 %all-to-all-start.1 = ((f32[128,8,256]{2,1,0:T(8,128)}), f32[128,8,256]{2,1,0:T(8,128)S(1)}, u32[]{:S(2)}, u32[]{:S(2)}) async-start(f32[128,8,256]{2,1,0:T(8,128)} %fusion.8), calls=%async_computation.1 | async-start | bytes 2097152 | tf_op jit(solution)/shard_map/all_to_all | solution.py:116
  83.4 0.1 add_cosine_fusion
  83.6 0.8 slice_bitcast_fusion.1
  84.3 18.0 %all-to-all-done.1 = f32[128,8,256]{2,1,0:T(8,128)S(1)} async-done(((f32[128,8,256]{2,1,0:T(8,128)}), f32[128,8,256]{2,1,0:T(8,128)S(1)}, u32[]{:S(2)}, u32[]{:S(2)}) %all-to-all-start.1) | async-done | bytes 1048608 | tf_op jit(solution)/shard_map/all_to_all | solution.py:116
  102.3 0.3 copy.82
  102.7 2.2 %fusion.5 = f32[1024,4,64]{0,2,1:T(8,128)S(1)} fusion(f32[4,64,1024]{2,1,0:T(8,128)S(1)} %bitcast.163, s32[1024]{0:T(1024)S(1)} %bitcast.183), kind=kOutput, calls=%fused_computation.7 | convolution fusion | flops 3222274048 | bytes 2101248 | tf_op jit(solution)/shard_map/kp,pm->km/dot_general | solution.py:18
  104.8 0.2 multiply_add_fusion
  105.0 2.0 %multiply_reduce_fusion.8 = (f32[2,4,64]{2,1,0:T(4,128)S(1)}, f32[2,256,4,64]{1,3,2,0:T(8,128)}) fusion(f32[2,256,64]{1,2,0:T(8,128)S(1)} %bitcast.152, f32[1024,1,64]{0,2,1:T(8,128)S(1)} %get-tuple-element.19, f32[1024,1,64]{0,2,1:T(8,128)S(1)} %get-tuple-element.18, f32[1024,1,64]{0,2,1:T(8,128)S(1)} %get-tuple-element.20, ...), kind=kOutput, calls=%fused_computation.52 | convolution fusion | flops 1612447232 | bytes 1851392 | tf_op jit(solution)/shard_map/nk,km->nm/dot_general | solution.py:18
  107.1 0.7 reshape.252
  107.8 3.5 %all-to-all-start.2 = ((f32[16,1,512]{2,1,0:T(1,128)}), f32[16,1,512]{2,1,0:T(1,128)S(1)}, u32[]{:S(2)}, u32[]{:S(2)}) async-start(f32[16,1,512]{2,1,0:T(1,128)} %reshape.252), calls=%async_computation.2 | async-start | bytes 65536 | tf_op jit(solution)/shard_map/all_to_all | solution.py:133
  111.3 7.6 %all-to-all-done.2 = f32[16,1,512]{2,1,0:T(1,128)S(1)} async-done(((f32[16,1,512]{2,1,0:T(1,128)}), f32[16,1,512]{2,1,0:T(1,128)S(1)}, u32[]{:S(2)}, u32[]{:S(2)}) %all-to-all-start.2) | async-done | bytes 32800 | tf_op jit(solution)/shard_map/all_to_all | solution.py:133
  118.9 0.5 broadcast.178
  119.4 0.6 reduce.4
  120.0 0.1 reshape.253
  120.2 59.8 %all-gather.5.cloned.1.call-done = f32[2,4096,256]{1,2,0:T(8,128)} async-done(((f32[2,256,256]{1,2,0:T(8,128)}), f32[2,4096,256]{1,2,0:T(8,128)}) %all-gather.5.cloned.1.call-update) | async-done | bytes 8388624 | tf_op jit(solution)/shard_map/all_gather | solution.py:135
  180.1 13.3 %fusion.59 = f32[2,256,256]{2,1,0:T(8,128)S(1)} fusion(f32[2,4096,256]{1,2,0:T(8,128)} %all-gather.5.cloned.1.call-done, f32[2,256,4096]{2,1,0:T(8,128)} %param.14), kind=kOutput, calls=%fused_computation.97 | convolution fusion | flops 3221225472 | bytes 17301504 | tf_op jit(solution)/shard_map/srj,sjm->srm/dot_general | solution.py:22
  193.4 0.1 multiply_subtract_fusion
  193.5 0.1 maximum_bitcast_fusion.2
  193.6 1.1 copy.84
  (68 shorter events, 1.4 us)
Async XLA Ops:
  6.5 52.6 %all-gather.3.cloned.1.call-start = ((), (), s32[]{:S(2)}) async-start(), calls=%async_computation.3 | async-start | bytes 2228224 | tf_op jit(solution)/shard_map/all_gather | solution.py:49
  8.0 14.1 %slice-start = ((s8[8388608]{0:T(1024)(128)(4,1)}), s8[4194304]{0:T(1024)(128)(4,1)S(1)}, s32[]{:S(2)}) async-start(s8[8388608]{0:T(1024)(128)(4,1)} %bitcast.148), calls=%async_computation.5 | async-start | bytes 8388608
  8.0 13.2 %copy-start.10 = (s32[1024]{0:T(1024)S(1)}, s32[1024]{0:T(1024)}, u32[]{:S(2)}) copy-start(s32[1024]{0:T(1024)} %param.20) | copy-start | bytes 12292
  8.0 14.0 %slice-start.1 = ((s8[8388608]{0:T(1024)(128)(4,1)}), s8[4194304]{0:T(1024)(128)(4,1)S(1)}, s32[]{:S(2)}) async-start(s8[8388608]{0:T(1024)(128)(4,1)} %bitcast.148), calls=%async_computation.6 | async-start | bytes 8388608
  8.0 14.0 %copy-start = (f32[2,64,256]{2,1,0:T(8,128)S(1)}, f32[2,64,256]{2,1,0:T(8,128)}, u32[]{:S(2)}) copy-start(f32[2,64,256]{2,1,0:T(8,128)} %param.15) | copy-start | bytes 393220
  8.1 14.0 %copy-start.8 = (s32[2,64]{1,0:T(2,128)S(1)}, s32[2,64]{1,0:T(2,128)}, u32[]{:S(2)}) copy-start(s32[2,64]{1,0:T(2,128)} %param.22) | copy-start | bytes 1540
  22.1 5.1 %copy-start.1 = (f32[2,256]{1,0:T(2,128)S(1)}, f32[2,256]{1,0:T(2,128)}, u32[]{:S(2)}) copy-start(f32[2,256]{1,0:T(2,128)} %param.16) | copy-start | bytes 6148
  22.1 14.5 %copy-start.5 = (s32[1,1024]{1,0:T(1,128)S(1)}, s32[1,1024]{1,0:T(1,128)}, u32[]{:S(2)}) copy-start(s32[1,1024]{1,0:T(1,128)} %param.21) | copy-start | bytes 12292
  26.9 11.3 %copy-start.2 = (f32[4]{0:T(128)S(1)}, f32[4]{0:T(128)}, u32[]{:S(2)}) copy-start(f32[4]{0:T(128)} %constant.8.clone) | copy-start | bytes 52
  26.9 11.4 %copy-start.3 = (f32[4]{0:T(128)S(1)}, f32[4]{0:T(128)}, u32[]{:S(2)}) copy-start(f32[4]{0:T(128)} %constant.26.clone) | copy-start | bytes 52
  26.9 11.6 %copy-start.4 = (f32[1024]{0:T(1024)S(1)}, f32[1024]{0:T(1024)}, u32[]{:S(2)}) copy-start(f32[1024]{0:T(1024)} %param.19) | copy-start | bytes 12292
  28.1 16.5 %all-to-all-start = ((f32[16,2,8,256]{3,2,1,0:T(8,128)}), f32[16,2,8,256]{3,2,1,0:T(8,128)S(1)}, u32[]{:S(2)}, u32[]{:S(2)}) async-start(f32[16,2,8,256]{3,2,1,0:T(8,128)} %broadcast_in_dim.23), calls=%async_computation | async-start | bytes 524288 | tf_op jit(solution)/shard_map/all_to_all | solution.py:84
  46.0 7.0 %copy-start.7 = (f32[2,64]{1,0:T(2,128)S(1)}, f32[2,64]{1,0:T(2,128)}, u32[]{:S(2)}) copy-start(f32[2,64]{1,0:T(2,128)} %param.24) | copy-start | bytes 1540
  46.0 7.0 %copy-start.6 = (s32[2,64]{1,0:T(2,128)S(1)}, s32[2,64]{1,0:T(2,128)}, u32[]{:S(2)}) copy-start(s32[2,64]{1,0:T(2,128)} %param.23) | copy-start | bytes 1540
  75.4 8.0 %copy-start.9 = (f32[4]{0:T(128)S(1)}, f32[4]{0:T(128)}, u32[]{:S(2)}) copy-start(f32[4]{0:T(128)} %constant.27.clone) | copy-start | bytes 52
  75.4 27.0 %all-to-all-start.1 = ((f32[128,8,256]{2,1,0:T(8,128)}), f32[128,8,256]{2,1,0:T(8,128)S(1)}, u32[]{:S(2)}, u32[]{:S(2)}) async-start(f32[128,8,256]{2,1,0:T(8,128)} %fusion.8), calls=%async_computation.1 | async-start | bytes 2097152 | tf_op jit(solution)/shard_map/all_to_all | solution.py:116
  83.3 96.8 %all-gather.5.cloned.1.call-start = ((), (), s32[]{:S(2)}) async-start(), calls=%async_computation.4 | async-start | bytes 8912896 | tf_op jit(solution)/shard_map/all_gather | solution.py:135
  107.8 11.1 %all-to-all-start.2 = ((f32[16,1,512]{2,1,0:T(1,128)}), f32[16,1,512]{2,1,0:T(1,128)S(1)}, u32[]{:S(2)}, u32[]{:S(2)}) async-start(f32[16,1,512]{2,1,0:T(1,128)} %reshape.252), calls=%async_computation.2 | async-start | bytes 65536 | tf_op jit(solution)/shard_map/all_to_all | solution.py:133
Sparse Core Ops, SparseCore 0:
  9.4 49.6 all-gather.2
  107.2 72.7 all-gather.4

commit v5 on v4

--- a/solution.py
+++ b/solution.py
@@ -16,6 +16,10 @@
 
 def mm(spec, a, b):
     return jnp.einsum(spec, a, b, precision=PRECISE, preferred_element_type=jnp.float32)
+
+
+def pick(spec, a, b):
+    return jnp.einsum(spec, a, b, precision=lax.Precision.HIGH, preferred_element_type=jnp.float32)
 
 
 def fast(spec, a, b):
@@ -105,16 +109,16 @@
     current0 = jnp.where(fault_step[:, None, :] <= t0[None, :, None], fault0 / denominator[:, None, :], 0.0)
     volt0 = open0 - current0[:, None] * fault_col[:, :, None, :]
 
-    at_ends = mm("kn,nm->km", attach_map, volt0.reshape(local, steps * cases)).reshape(ends, steps, cases)
+    at_ends = pick("kn,nm->km", attach_map, volt0.reshape(local, steps * cases)).reshape(ends, steps, cases)
     waves = 2.0 * conductance[:, None, None] * at_ends - jnp.transpose(base[:steps])[:, :, None]
 
     slot_row = pair_slot[0]
     end_ids = lax.iota(jnp.int32, ends)
     selector = (end_ids[:, None] == slot_row[None, :]).astype(jnp.float32)
     selectorT = (slot_row[:, None] == end_ids[None, :]).astype(jnp.float32)
-    outgoing = mm("pk,km->pm", selectorT, waves.reshape(ends, steps * cases))
+    outgoing = pick("pk,km->pm", selectorT, waves.reshape(ends, steps * cases))
     incoming = lax.all_to_all(outgoing, ("region", "node"), 0, 0, tiled=True)
-    far = mm("kp,pm->km", selector, incoming).reshape(ends, steps, cases)
+    far = pick("kp,pm->km", selector, incoming).reshape(ends, steps, cases)
 
     taps_t = jnp.transpose(impulse_taps[:steps])
     base_t = jnp.transpose(base[steps:])
@@ -125,7 +129,7 @@
             history = history + taps_t[:, j][:, None] * far[:, t - steps - j]
         hist_list.append(history)
     hist1 = jnp.stack(hist_list, axis=1).reshape(ends, steps * cases)
-    node_hist = mm("nk,km->nm", attach_mapT, hist1).reshape(subnets, rows, steps, cases)
+    node_hist = pick("nk,km->nm", attach_mapT, hist1).reshape(subnets, rows, steps, cases)
     angle1 = jnp.asarray(omega_step * np.arange(steps, total), jnp.float32)
     phase = jnp.cos(angle1[None, None, :] + source_angle[:, :, None])
     inj1 = amp_t[:, :, None, :] * phase[:, :, :, None] + node_hist

time: 202 us -> 199 us (0.985)
  matrix products: 55.8 us -> 53.2 us
    dot_general x8 -> x4, matrix products: 28.1 us -> 18.9 us  [mm(): jnp.einsum(spec, a, b, precision=PRECISE, preferred_element_type=jnp.floa...]
    dot_general x0 -> x4, matrix products: none -> 6.62 us  [pick(): jnp.einsum(spec, a, b, precision=lax.Precision.HIGH, preferred_element_ty...]
where the time goes in v5:
time: 199 us
  waiting for transfers between devices  98.4 us (49%)
  matrix products  53.2 us (27%)
  starting transfers between devices  19.4 us (10%)
  between operations  13.9 us (7%)
  local copies, waits for them, and re-layouts  8.51 us (4%)
  other arithmetic  5.42 us (3%)
    all_gather x1, waiting for transfers between devices, body(): lax.all_gather(inj1.reshape(subnets, rows, steps * cases), 'node', axis=1...  59.8 us
    dot_general x3, matrix products, fast(): jnp.einsum(spec, a, b, precision=lax.Precision.HIGH, preferred_element_ty...  27.7 us
    dot_general x4, matrix products, mm(): jnp.einsum(spec, a, b, precision=PRECISE, preferred_element_type=jnp.floa...  18.9 us
    all_to_all x1, waiting for transfers between devices, body(): incoming = lax.all_to_all(outgoing, ('region', 'node'), 0, 0, tiled=True)  18 us
    all_to_all x1, starting transfers between devices, body(): small = lax.all_to_all(small, 'node', 0, 0, tiled=True)  8 us
    all_to_all x1, starting transfers between devices, body(): incoming = lax.all_to_all(outgoing, ('region', 'node'), 0, 0, tiled=True)  7.93 us
    all_to_all x1, waiting for transfers between devices, body(): lax.all_to_all(jnp.broadcast_to(part1[None], (n_node,) + part1.shape), 'n...  7.55 us
    dot_general x4, matrix products, pick(): jnp.einsum(spec, a, b, precision=lax.Precision.HIGH, preferred_element_ty...  6.62 us
  transfers between devices with their start and end apart: 5, of which 5 were waited for; matrix products, arithmetic and copies ran while one was open for 17% of the time, Pallas kernels for 0%

profile of v5, /device:TPU:0, one launch (start us, length us, event | category | flops | bytes accessed | tf_op | source)
XLA Modules:
  0.0 198.9 jit_solution(4633955475333885623)
XLA Ops:
  6.5 0.7 all-gather.3.cloned.1.call-update
  7.3 0.7 fusion.57
  8.1 13.1 %multiply_reduce_fusion.3 = (f32[1024]{0:T(1024)S(1)}, f32[1024]{0:T(1024)S(1)}, f32[1024]{0:T(1024)S(1)}, f32[1024]{0:T(1024)S(1)}, f32[1024]{0:T(1024)S(1)}, /...) fusion(f32[515,1024]{1,0:T(8,128)} %param.18, f32[512,1024]{1,0:T(8,128)} %param.17), kind=kOutput, calls=%fused_computation.15 | convolution fusion | flops 3230130176 | bytes 12648448 | tf_op jit(solution)/shard_map/uj,jk->uk/dot_general | solution.py:18
  21.2 0.8 fusion.12
  22.1 4.7 %multiply_reduce_fusion.10 = (f32[2,64]{1,0:T(2,128)S(1)}, f32[2,64]{1,0:T(2,128)S(1)}, f32[2,64]{1,0:T(2,128)S(1)}, f32[2,64,256]{2,1,0:T(8,128)S(1)}) fusion(f32[2,256]{1,0:T(2,128)S(1)} %get-tuple-element.40, f32[2,64,256]{2,1,0:T(8,128)S(1)} %copy-done, f32[2,256]{1,0:T(2,128)S(1)} %get-tuple-element.39, s32[2,64]{1,0:T(2,128)S(1)} %copy-done.8, ...), kind=kOutput, calls=%fused_computation.68 | convolution fusion | flops 1611431552 | bytes 8657920 | tf_op jit(solution)/shard_map/srj,sjc->src/dot_general | solution.py:18
  26.9 0.2 fusion.58
  27.4 0.7 broadcast_in_dim.23
  28.1 8.0 %all-to-all-start = ((f32[16,2,8,256]{3,2,1,0:T(8,128)}), f32[16,2,8,256]{3,2,1,0:T(8,128)S(1)}, u32[]{:S(2)}, u32[]{:S(2)}) async-start(f32[16,2,8,256]{3,2,1,0:T(8,128)} %broadcast_in_dim.23), calls=%async_computation | async-start | bytes 524288 | tf_op jit(solution)/shard_map/all_to_all | solution.py:88
  36.1 0.5 broadcast.177
  36.7 0.6 reduce.3
  37.3 0.1 eq.136
  37.4 0.7 fusion.7
  38.2 0.1 mul.331
  38.5 6.2 %all-to-all-done = f32[16,2,8,256]{3,2,1,0:T(8,128)S(1)} async-done(((f32[16,2,8,256]{3,2,1,0:T(8,128)}), f32[16,2,8,256]{3,2,1,0:T(8,128)S(1)}, u32[]{:S(2)}, u32[]{:S(2)}) %all-to-all-start) | async-done | bytes 262176 | tf_op jit(solution)/shard_map/all_to_all | solution.py:88
  44.6 1.0 slice_cosine_fusion
  45.9 6.7 %convolution_bitcast_fusion = f32[2,256,4]{1,2,0:T(4,128)S(1)} fusion(f32[2,4096,4]{1,2,0:T(4,128)S(1)} %bitcast.165, f32[2,256,4096]{2,1,0:T(8,128)} %param.14), kind=kOutput, calls=%fused_computation.33 | convolution fusion | flops 50331648 | bytes 8527872 | tf_op jit(solution)/shard_map/srj,sjt->srt/dot_general | solution.py:26
  52.6 0.1 add.142.clone
  52.9 6.2 %all-gather.3.cloned.1.call-done = f32[2,64,4096]{2,1,0:T(8,128)} async-done(((f32[2,64,256]{2,1,0:T(8,128)}), f32[2,64,4096]{2,1,0:T(8,128)}) %all-gather.3.cloned.1.call-update) | async-done | bytes 2097168 | tf_op jit(solution)/shard_map/all_gather | solution.py:53
  59.1 2.1 %broadcast_multiply_fusion.1 = (f32[2,64,4096]{2,1,0:T(8,128)S(1)}, f32[2,64,4096]{2,1,0:T(8,128)S(1)}) fusion(f32[2,64,4096]{2,1,0:T(8,128)} %all-gather.3.cloned.1.call-done, f32[2,4096]{1,0:T(2,128)S(1)} %bitcast.168, f32[2,4096]{1,0:T(2,128)S(1)} %bitcast.169), kind=kLoop, calls=%fused_computation.45 | loop fusion | flops 1048576 | bytes 6356992 | tf_op jit(solution)/shard_map/mul | solution.py:93
  61.3 7.6 %fusion.28 = f32[2,256,128]{1,2,0:T(8,128)S(1)} fusion(f32[2,256,4096]{2,1,0:T(8,128)} %param.14, f32[2,64,4096]{2,1,0:T(8,128)S(1)} %get-tuple-element.17, f32[2,64,4096]{2,1,0:T(8,128)S(1)} %get-tuple-element.16), kind=kOutput, calls=%fused_computation.32 | convolution fusion | flops 1611661312 | bytes 12845056 | tf_op jit(solution)/shard_map/srj,scj->src/dot_general | solution.py:26
  68.9 0.1 copy.93
  69.0 0.1 copy.94
  69.2 0.2 add_subtract_fusion.1
  69.3 0.4 copy.79
  69.8 0.1 mul.303.clone
  70.0 0.1 mul.306.clone
  70.2 0.2 add_subtract_fusion
  70.4 1.0 fusion.22
  71.3 2.3 %fusion.8 = f32[128,8,256]{2,1,0:T(8,128)} fusion(f32[1024,256,1]{0,1,2:T(8,128)S(1)} %bitcast.202, pred[128,8,1024]{2,0,1:T(32,128)(4,1)S(1)} %fusion.7), kind=kOutput, calls=%fused_computation.9 | convolution fusion | flops 1610612736 | bytes 3145728 | tf_op jit(solution)/shard_map/pk,km->pm/dot_general | solution.py:22
  73.7 7.9 %all-to-all-start.1 = ((f32[128,8,256]{2,1,0:T(8,128)}), f32[128,8,256]{2,1,0:T(8,128)S(1)}, u32[]{:S(2)}, u32[]{:S(2)}) async-start(f32[128,8,256]{2,1,0:T(8,128)} %fusion.8), calls=%async_computation.1 | async-start | bytes 2097152 | tf_op jit(solution)/shard_map/all_to_all | solution.py:120
  81.7 0.1 add_cosine_fusion
  81.9 0.8 slice_bitcast_fusion.1
  82.6 18.0 %all-to-all-done.1 = f32[128,8,256]{2,1,0:T(8,128)S(1)} async-done(((f32[128,8,256]{2,1,0:T(8,128)}), f32[128,8,256]{2,1,0:T(8,128)S(1)}, u32[]{:S(2)}, u32[]{:S(2)}) %all-to-all-start.1) | async-done | bytes 1048608 | tf_op jit(solution)/shard_map/all_to_all | solution.py:120
  100.6 0.3 copy.82
  101.0 1.6 fusion.5
  102.6 0.2 multiply_add_fusion
  102.8 1.7 multiply_reduce_fusion.8
  104.5 0.7 reshape.252
  105.2 3.5 %all-to-all-start.2 = ((f32[16,1,512]{2,1,0:T(1,128)}), f32[16,1,512]{2,1,0:T(1,128)S(1)}, u32[]{:S(2)}, u32[]{:S(2)}) async-start(f32[16,1,512]{2,1,0:T(1,128)} %reshape.252), calls=%async_computation.2 | async-start | bytes 65536 | tf_op jit(solution)/shard_map/all_to_all | solution.py:137
  108.7 7.6 %all-to-all-done.2 = f32[16,1,512]{2,1,0:T(1,128)S(1)} async-done(((f32[16,1,512]{2,1,0:T(1,128)}), f32[16,1,512]{2,1,0:T(1,128)S(1)}, u32[]{:S(2)}, u32[]{:S(2)}) %all-to-all-start.2) | async-done | bytes 32800 | tf_op jit(solution)/shard_map/all_to_all | solution.py:137
  116.3 0.5 broadcast.178
  116.8 0.6 reduce.4
  117.4 0.1 reshape.253
  117.6 59.8 %all-gather.5.cloned.1.call-done = f32[2,4096,256]{1,2,0:T(8,128)} async-done(((f32[2,256,256]{1,2,0:T(8,128)}), f32[2,4096,256]{1,2,0:T(8,128)}) %all-gather.5.cloned.1.call-update) | async-done | bytes 8388624 | tf_op jit(solution)/shard_map/all_gather | solution.py:139
  177.5 13.3 %fusion.59 = f32[2,256,256]{2,1,0:T(8,128)S(1)} fusion(f32[2,4096,256]{1,2,0:T(8,128)} %all-gather.5.cloned.1.call-done, f32[2,256,4096]{2,1,0:T(8,128)} %param.14), kind=kOutput, calls=%fused_computation.97 | convolution fusion | flops 3221225472 | bytes 17301504 | tf_op jit(solution)/shard_map/srj,sjm->srm/dot_general | solution.py:26
  190.8 0.1 multiply_subtract_fusion
  190.9 0.1 maximum_bitcast_fusion.2
  191.0 1.1 copy.84
  (68 shorter events, 1.4 us)
Async XLA Ops:
  6.5 52.6 %all-gather.3.cloned.1.call-start = ((), (), s32[]{:S(2)}) async-start(), calls=%async_computation.3 | async-start | bytes 2228224 | tf_op jit(solution)/shard_map/all_gather | solution.py:53
  8.0 14.1 %slice-start = ((s8[8388608]{0:T(1024)(128)(4,1)}), s8[4194304]{0:T(1024)(128)(4,1)S(1)}, s32[]{:S(2)}) async-start(s8[8388608]{0:T(1024)(128)(4,1)} %bitcast.148), calls=%async_computation.5 | async-start | bytes 8388608
  8.0 13.2 %copy-start.10 = (s32[1024]{0:T(1024)S(1)}, s32[1024]{0:T(1024)}, u32[]{:S(2)}) copy-start(s32[1024]{0:T(1024)} %param.20) | copy-start | bytes 12292
  8.0 14.0 %slice-start.1 = ((s8[8388608]{0:T(1024)(128)(4,1)}), s8[4194304]{0:T(1024)(128)(4,1)S(1)}, s32[]{:S(2)}) async-start(s8[8388608]{0:T(1024)(128)(4,1)} %bitcast.148), calls=%async_computation.6 | async-start | bytes 8388608
  8.0 14.0 %copy-start = (f32[2,64,256]{2,1,0:T(8,128)S(1)}, f32[2,64,256]{2,1,0:T(8,128)}, u32[]{:S(2)}) copy-start(f32[2,64,256]{2,1,0:T(8,128)} %param.15) | copy-start | bytes 393220
  8.1 14.0 %copy-start.8 = (s32[2,64]{1,0:T(2,128)S(1)}, s32[2,64]{1,0:T(2,128)}, u32[]{:S(2)}) copy-start(s32[2,64]{1,0:T(2,128)} %param.22) | copy-start | bytes 1540
  22.1 5.1 %copy-start.1 = (f32[2,256]{1,0:T(2,128)S(1)}, f32[2,256]{1,0:T(2,128)}, u32[]{:S(2)}) copy-start(f32[2,256]{1,0:T(2,128)} %param.16) | copy-start | bytes 6148
  22.1 14.5 %copy-start.5 = (s32[1,1024]{1,0:T(1,128)S(1)}, s32[1,1024]{1,0:T(1,128)}, u32[]{:S(2)}) copy-start(s32[1,1024]{1,0:T(1,128)} %param.21) | copy-start | bytes 12292
  26.9 11.3 %copy-start.2 = (f32[4]{0:T(128)S(1)}, f32[4]{0:T(128)}, u32[]{:S(2)}) copy-start(f32[4]{0:T(128)} %constant.8.clone) | copy-start | bytes 52
  26.9 11.4 %copy-start.3 = (f32[4]{0:T(128)S(1)}, f32[4]{0:T(128)}, u32[]{:S(2)}) copy-start(f32[4]{0:T(128)} %constant.26.clone) | copy-start | bytes 52
  26.9 11.6 %copy-start.4 = (f32[1024]{0:T(1024)S(1)}, f32[1024]{0:T(1024)}, u32[]{:S(2)}) copy-start(f32[1024]{0:T(1024)} %param.19) | copy-start | bytes 12292
  28.1 16.5 %all-to-all-start = ((f32[16,2,8,256]{3,2,1,0:T(8,128)}), f32[16,2,8,256]{3,2,1,0:T(8,128)S(1)}, u32[]{:S(2)}, u32[]{:S(2)}) async-start(f32[16,2,8,256]{3,2,1,0:T(8,128)} %broadcast_in_dim.23), calls=%async_computation | async-start | bytes 524288 | tf_op jit(solution)/shard_map/all_to_all | solution.py:88
  45.8 7.0 %copy-start.7 = (f32[2,64]{1,0:T(2,128)S(1)}, f32[2,64]{1,0:T(2,128)}, u32[]{:S(2)}) copy-start(f32[2,64]{1,0:T(2,128)} %param.24) | copy-start | bytes 1540
  45.9 7.0 %copy-start.6 = (s32[2,64]{1,0:T(2,128)S(1)}, s32[2,64]{1,0:T(2,128)}, u32[]{:S(2)}) copy-start(s32[2,64]{1,0:T(2,128)} %param.23) | copy-start | bytes 1540
  73.7 8.0 %copy-start.9 = (f32[4]{0:T(128)S(1)}, f32[4]{0:T(128)}, u32[]{:S(2)}) copy-start(f32[4]{0:T(128)} %constant.27.clone) | copy-start | bytes 52
  73.7 27.0 %all-to-all-start.1 = ((f32[128,8,256]{2,1,0:T(8,128)}), f32[128,8,256]{2,1,0:T(8,128)S(1)}, u32[]{:S(2)}, u32[]{:S(2)}) async-start(f32[128,8,256]{2,1,0:T(8,128)} %fusion.8), calls=%async_computation.1 | async-start | bytes 2097152 | tf_op jit(solution)/shard_map/all_to_all | solution.py:120
  81.6 95.9 %all-gather.5.cloned.1.call-start = ((), (), s32[]{:S(2)}) async-start(), calls=%async_computation.4 | async-start | bytes 8912896 | tf_op jit(solution)/shard_map/all_gather | solution.py:139
  105.2 11.0 %all-to-all-start.2 = ((f32[16,1,512]{2,1,0:T(1,128)}), f32[16,1,512]{2,1,0:T(1,128)S(1)}, u32[]{:S(2)}, u32[]{:S(2)}) async-start(f32[16,1,512]{2,1,0:T(1,128)} %reshape.252), calls=%async_computation.2 | async-start | bytes 65536 | tf_op jit(solution)/shard_map/all_to_all | solution.py:137
Sparse Core Ops, SparseCore 0:
  9.4 49.6 all-gather.2
  104.6 72.7 all-gather.4

commit v6 on v5

--- a/solution.py
+++ b/solution.py
@@ -116,9 +116,9 @@
     end_ids = lax.iota(jnp.int32, ends)
     selector = (end_ids[:, None] == slot_row[None, :]).astype(jnp.float32)
     selectorT = (slot_row[:, None] == end_ids[None, :]).astype(jnp.float32)
-    outgoing = pick("pk,km->pm", selectorT, waves.reshape(ends, steps * cases))
-    incoming = lax.all_to_all(outgoing, ("region", "node"), 0, 0, tiled=True)
-    far = pick("kp,pm->km", selector, incoming).reshape(ends, steps, cases)
+    outgoing = pick("pk,km->mp", selectorT, waves.reshape(ends, steps * cases))
+    incoming = lax.all_to_all(outgoing, ("region", "node"), 1, 1, tiled=True)
+    far = pick("kp,mp->km", selector, incoming).reshape(ends, steps, cases)
 
     taps_t = jnp.transpose(impulse_taps[:steps])
     base_t = jnp.transpose(base[steps:])

time: 199 us -> 201 us (1.010)
  no operation moved by 1% of the time
where the time goes in v6:
time: 201 us; the launch traced here: 200 us
  waiting for transfers between devices  98.3 us (49%)
  matrix products  53.1 us (26%)
  starting transfers between devices  19.4 us (10%)
  between operations  13.9 us (7%)
  local copies, waits for them, and re-layouts  9.13 us (5%)
  other arithmetic  6.37 us (3%)
    all_gather x1, waiting for transfers between devices, body(): lax.all_gather(inj1.reshape(subnets, rows, steps * cases), 'node', axis=1...  59.7 us
    dot_general x3, matrix products, fast(): jnp.einsum(spec, a, b, precision=lax.Precision.HIGH, preferred_element_ty...  27.7 us
    dot_general x4, matrix products, mm(): jnp.einsum(spec, a, b, precision=PRECISE, preferred_element_type=jnp.floa...  18.9 us
    all_to_all x1, waiting for transfers between devices, body(): incoming = lax.all_to_all(outgoing, ('region', 'node'), 1, 1, tiled=True)  18 us
    all_to_all x1, starting transfers between devices, body(): small = lax.all_to_all(small, 'node', 0, 0, tiled=True)  8 us
    all_to_all x1, starting transfers between devices, body(): incoming = lax.all_to_all(outgoing, ('region', 'node'), 1, 1, tiled=True)  7.93 us
    all_to_all x1, waiting for transfers between devices, body(): lax.all_to_all(jnp.broadcast_to(part1[None], (n_node,) + part1.shape), 'n...  7.55 us
    dot_general x4, matrix products, pick(): jnp.einsum(spec, a, b, precision=lax.Precision.HIGH, preferred_element_ty...  6.53 us
  transfers between devices with their start and end apart: 5, of which 5 were waited for; matrix products, arithmetic and copies ran while one was open for 17% of the time, Pallas kernels for 0%

profile of v6, /device:TPU:0, one launch (start us, length us, event | category | flops | bytes accessed | tf_op | source)
XLA Modules:
  0.0 200.3 jit_solution(918163848191744240)
XLA Ops:
  6.5 0.7 all-gather.3.cloned.1.call-update
  7.3 0.7 fusion.58
  8.1 13.1 %multiply_reduce_fusion.3 = (f32[1024]{0:T(1024)S(1)}, f32[1024]{0:T(1024)S(1)}, f32[1024]{0:T(1024)S(1)}, f32[1024]{0:T(1024)S(1)}, f32[1024]{0:T(1024)S(1)}, /...) fusion(f32[515,1024]{1,0:T(8,128)} %param.18, f32[512,1024]{1,0:T(8,128)} %param.17), kind=kOutput, calls=%fused_computation.16 | convolution fusion | flops 3230130176 | bytes 12648448 | tf_op jit(solution)/shard_map/uj,jk->uk/dot_general | solution.py:18
  21.2 0.8 fusion.13
  22.1 4.7 %multiply_reduce_fusion.10 = (f32[2,64]{1,0:T(2,128)S(1)}, f32[2,64]{1,0:T(2,128)S(1)}, f32[2,64]{1,0:T(2,128)S(1)}, f32[2,64,256]{2,1,0:T(8,128)S(1)}) fusion(f32[2,256]{1,0:T(2,128)S(1)} %get-tuple-element.40, f32[2,64,256]{2,1,0:T(8,128)S(1)} %copy-done.1, f32[2,256]{1,0:T(2,128)S(1)} %get-tuple-element.39, s32[2,64]{1,0:T(2,128)S(1)} %copy-done.9, ...), kind=kOutput, calls=%fused_computation.69 | convolution fusion | flops 1611431552 | bytes 8657920 | tf_op jit(solution)/shard_map/srj,sjc->src/dot_general | solution.py:18
  26.9 0.2 fusion.59
  27.4 0.7 broadcast_in_dim.23
  28.1 8.0 %all-to-all-start = ((f32[16,2,8,256]{3,2,1,0:T(8,128)}), f32[16,2,8,256]{3,2,1,0:T(8,128)S(1)}, u32[]{:S(2)}, u32[]{:S(2)}) async-start(f32[16,2,8,256]{3,2,1,0:T(8,128)} %broadcast_in_dim.23), calls=%async_computation | async-start | bytes 524288 | tf_op jit(solution)/shard_map/all_to_all | solution.py:88
  36.1 0.5 broadcast.177
  36.7 0.6 reduce.3
  37.3 0.1 eq.136
  37.4 0.7 fusion.7
  38.2 0.1 mul.331
  38.5 6.2 %all-to-all-done = f32[16,2,8,256]{3,2,1,0:T(8,128)S(1)} async-done(((f32[16,2,8,256]{3,2,1,0:T(8,128)}), f32[16,2,8,256]{3,2,1,0:T(8,128)S(1)}, u32[]{:S(2)}, u32[]{:S(2)}) %all-to-all-start) | async-done | bytes 262176 | tf_op jit(solution)/shard_map/all_to_all | solution.py:88
  44.6 1.0 slice_cosine_fusion
  45.9 6.7 %convolution_bitcast_fusion = f32[2,256,4]{1,2,0:T(4,128)S(1)} fusion(f32[2,4096,4]{1,2,0:T(4,128)S(1)} %bitcast.160, f32[2,256,4096]{2,1,0:T(8,128)} %param.14), kind=kOutput, calls=%fused_computation.34 | convolution fusion | flops 50331648 | bytes 8527872 | tf_op jit(solution)/shard_map/srj,sjt->srt/dot_general | solution.py:26
  52.6 0.1 add.142.clone
  52.9 6.2 %all-gather.3.cloned.1.call-done = f32[2,64,4096]{2,1,0:T(8,128)} async-done(((f32[2,64,256]{2,1,0:T(8,128)}), f32[2,64,4096]{2,1,0:T(8,128)}) %all-gather.3.cloned.1.call-update) | async-done | bytes 2097168 | tf_op jit(solution)/shard_map/all_gather | solution.py:53
  59.1 2.1 %broadcast_multiply_fusion.1 = (f32[2,64,4096]{2,1,0:T(8,128)S(1)}, f32[2,64,4096]{2,1,0:T(8,128)S(1)}) fusion(f32[2,64,4096]{2,1,0:T(8,128)} %all-gather.3.cloned.1.call-done, f32[2,4096]{1,0:T(2,128)S(1)} %bitcast.163, f32[2,4096]{1,0:T(2,128)S(1)} %bitcast.164), kind=kLoop, calls=%fused_computation.46 | loop fusion | flops 1048576 | bytes 6356992 | tf_op jit(solution)/shard_map/mul | solution.py:93
  61.3 7.7 %fusion.29 = f32[2,256,128]{1,2,0:T(8,128)S(1)} fusion(f32[2,256,4096]{2,1,0:T(8,128)} %param.14, f32[2,64,4096]{2,1,0:T(8,128)S(1)} %get-tuple-element.17, f32[2,64,4096]{2,1,0:T(8,128)S(1)} %get-tuple-element.16), kind=kOutput, calls=%fused_computation.33 | convolution fusion | flops 1611661312 | bytes 12845056 | tf_op jit(solution)/shard_map/srj,scj->src/dot_general | solution.py:26
  68.9 0.1 copy.86
  69.0 0.1 copy.87
  69.2 1.0 add_subtract_fusion.1
  70.2 0.4 copy.74
  70.6 0.1 mul.303.clone
  70.8 0.1 mul.306.clone
  71.0 0.2 add_subtract_fusion
  71.2 1.0 fusion.23
  72.2 2.3 %fusion.8 = f32[256,128,8]{0,2,1:T(8,128)} fusion(f32[1024,256,1]{0,1,2:T(8,128)S(1)} %bitcast.197, pred[128,8,1024]{2,0,1:T(32,128)(4,1)S(1)} %fusion.7), kind=kOutput, calls=%fused_computation.9 | convolution fusion | flops 1610612736 | bytes 3145728 | tf_op jit(solution)/shard_map/pk,km->mp/dot_general | solution.py:22
  74.5 7.9 %all-to-all-start.1 = ((f32[256,128,8]{0,2,1:T(8,128)}), f32[256,128,8]{0,2,1:T(8,128)S(1)}, u32[]{:S(2)}, u32[]{:S(2)}) async-start(f32[256,128,8]{0,2,1:T(8,128)} %fusion.8), calls=%async_computation.1 | async-start | bytes 2097152 | tf_op jit(solution)/shard_map/all_to_all | solution.py:120
  82.5 0.1 add_cosine_fusion
  82.7 0.8 slice_bitcast_fusion.1
  83.5 18.0 %all-to-all-done.1 = f32[256,128,8]{0,2,1:T(8,128)S(1)} async-done(((f32[256,128,8]{0,2,1:T(8,128)}), f32[256,128,8]{0,2,1:T(8,128)S(1)}, u32[]{:S(2)}, u32[]{:S(2)}) %all-to-all-start.1) | async-done | bytes 1048608 | tf_op jit(solution)/shard_map/all_to_all | solution.py:120
  101.4 0.9 dot_general.64
  102.3 1.6 fusion.5
  103.9 0.2 multiply_add_fusion
  104.1 1.7 multiply_reduce_fusion.8
  105.9 0.7 reshape.253
  106.6 3.5 %all-to-all-start.2 = ((f32[16,1,512]{2,1,0:T(1,128)}), f32[16,1,512]{2,1,0:T(1,128)S(1)}, u32[]{:S(2)}, u32[]{:S(2)}) async-start(f32[16,1,512]{2,1,0:T(1,128)} %reshape.253), calls=%async_computation.2 | async-start | bytes 65536 | tf_op jit(solution)/shard_map/all_to_all | solution.py:137
  110.1 7.6 %all-to-all-done.2 = f32[16,1,512]{2,1,0:T(1,128)S(1)} async-done(((f32[16,1,512]{2,1,0:T(1,128)}), f32[16,1,512]{2,1,0:T(1,128)S(1)}, u32[]{:S(2)}, u32[]{:S(2)}) %all-to-all-start.2) | async-done | bytes 32800 | tf_op jit(solution)/shard_map/all_to_all | solution.py:137
  117.7 0.5 broadcast.178
  118.2 0.7 reduce.4
  118.9 0.1 reshape.254
  119.1 59.7 %all-gather.5.cloned.1.call-done = f32[2,4096,256]{1,2,0:T(8,128)} async-done(((f32[2,256,256]{1,2,0:T(8,128)}), f32[2,4096,256]{1,2,0:T(8,128)}) %all-gather.5.cloned.1.call-update) | async-done | bytes 8388624 | tf_op jit(solution)/shard_map/all_gather | solution.py:139
  178.8 13.3 %fusion.60 = f32[2,256,256]{2,1,0:T(8,128)S(1)} fusion(f32[2,4096,256]{1,2,0:T(8,128)} %all-gather.5.cloned.1.call-done, f32[2,256,4096]{2,1,0:T(8,128)} %param.14), kind=kOutput, calls=%fused_computation.98 | convolution fusion | flops 3221225472 | bytes 17301504 | tf_op jit(solution)/shard_map/srj,sjm->srm/dot_general | solution.py:26
  192.1 0.1 multiply_subtract_fusion
  192.3 0.1 maximum_bitcast_fusion.2
  192.4 1.1 copy.79
  (70 shorter events, 1.4 us)
Async XLA Ops:
  6.5 52.6 %all-gather.3.cloned.1.call-start = ((), (), s32[]{:S(2)}) async-start(), calls=%async_computation.3 | async-start | bytes 2228224 | tf_op jit(solution)/shard_map/all_gather | solution.py:53
  8.0 14.1 %slice-start = ((s8[8388608]{0:T(1024)(128)(4,1)}), s8[4194304]{0:T(1024)(128)(4,1)S(1)}, s32[]{:S(2)}) async-start(s8[8388608]{0:T(1024)(128)(4,1)} %bitcast.145), calls=%async_computation.5 | async-start | bytes 8388608
  8.0 13.2 %copy-start.11 = (s32[1024]{0:T(1024)S(1)}, s32[1024]{0:T(1024)}, u32[]{:S(2)}) copy-start(s32[1024]{0:T(1024)} %param.20) | copy-start | bytes 12292
  8.0 14.0 %slice-start.1 = ((s8[8388608]{0:T(1024)(128)(4,1)}), s8[4194304]{0:T(1024)(128)(4,1)S(1)}, s32[]{:S(2)}) async-start(s8[8388608]{0:T(1024)(128)(4,1)} %bitcast.145), calls=%async_computation.6 | async-start | bytes 8388608
  8.0 14.0 %copy-start.1 = (f32[2,64,256]{2,1,0:T(8,128)S(1)}, f32[2,64,256]{2,1,0:T(8,128)}, u32[]{:S(2)}) copy-start(f32[2,64,256]{2,1,0:T(8,128)} %param.15) | copy-start | bytes 393220
  8.1 14.0 %copy-start.9 = (s32[2,64]{1,0:T(2,128)S(1)}, s32[2,64]{1,0:T(2,128)}, u32[]{:S(2)}) copy-start(s32[2,64]{1,0:T(2,128)} %param.22) | copy-start | bytes 1540
  22.1 5.1 %copy-start.2 = (f32[2,256]{1,0:T(2,128)S(1)}, f32[2,256]{1,0:T(2,128)}, u32[]{:S(2)}) copy-start(f32[2,256]{1,0:T(2,128)} %param.16) | copy-start | bytes 6148
  22.1 14.5 %copy-start.6 = (s32[1,1024]{1,0:T(1,128)S(1)}, s32[1,1024]{1,0:T(1,128)}, u32[]{:S(2)}) copy-start(s32[1,1024]{1,0:T(1,128)} %param.21) | copy-start | bytes 12292
  26.9 11.3 %copy-start.3 = (f32[4]{0:T(128)S(1)}, f32[4]{0:T(128)}, u32[]{:S(2)}) copy-start(f32[4]{0:T(128)} %constant.8.clone) | copy-start | bytes 52
  26.9 11.4 %copy-start.4 = (f32[4]{0:T(128)S(1)}, f32[4]{0:T(128)}, u32[]{:S(2)}) copy-start(f32[4]{0:T(128)} %constant.26.clone) | copy-start | bytes 52
  26.9 11.6 %copy-start.5 = (f32[1024]{0:T(1024)S(1)}, f32[1024]{0:T(1024)}, u32[]{:S(2)}) copy-start(f32[1024]{0:T(1024)} %param.19) | copy-start | bytes 12292
  28.1 16.5 %all-to-all-start = ((f32[16,2,8,256]{3,2,1,0:T(8,128)}), f32[16,2,8,256]{3,2,1,0:T(8,128)S(1)}, u32[]{:S(2)}, u32[]{:S(2)}) async-start(f32[16,2,8,256]{3,2,1,0:T(8,128)} %broadcast_in_dim.23), calls=%async_computation | async-start | bytes 524288 | tf_op jit(solution)/shard_map/all_to_all | solution.py:88
  45.8 7.0 %copy-start.8 = (f32[2,64]{1,0:T(2,128)S(1)}, f32[2,64]{1,0:T(2,128)}, u32[]{:S(2)}) copy-start(f32[2,64]{1,0:T(2,128)} %param.24) | copy-start | bytes 1540
  45.9 7.0 %copy-start.7 = (s32[2,64]{1,0:T(2,128)S(1)}, s32[2,64]{1,0:T(2,128)}, u32[]{:S(2)}) copy-start(s32[2,64]{1,0:T(2,128)} %param.23) | copy-start | bytes 1540
  74.5 8.0 %copy-start.10 = (f32[4]{0:T(128)S(1)}, f32[4]{0:T(128)}, u32[]{:S(2)}) copy-start(f32[4]{0:T(128)} %constant.27.clone) | copy-start | bytes 52
  74.5 27.0 %all-to-all-start.1 = ((f32[256,128,8]{0,2,1:T(8,128)}), f32[256,128,8]{0,2,1:T(8,128)S(1)}, u32[]{:S(2)}, u32[]{:S(2)}) async-start(f32[256,128,8]{0,2,1:T(8,128)} %fusion.8), calls=%async_computation.1 | async-start | bytes 2097152 | tf_op jit(solution)/shard_map/all_to_all | solution.py:120
  82.4 96.4 %all-gather.5.cloned.1.call-start = ((), (), s32[]{:S(2)}) async-start(), calls=%async_computation.4 | async-start | bytes 8912896 | tf_op jit(solution)/shard_map/all_gather | solution.py:139
  106.6 11.1 %all-to-all-start.2 = ((f32[16,1,512]{2,1,0:T(1,128)}), f32[16,1,512]{2,1,0:T(1,128)S(1)}, u32[]{:S(2)}, u32[]{:S(2)}) async-start(f32[16,1,512]{2,1,0:T(1,128)} %reshape.253), calls=%async_computation.2 | async-start | bytes 65536 | tf_op jit(solution)/shard_map/all_to_all | solution.py:137
  119.1 73.2 %copy-start = (f32[2,256,4,64]{1,3,2,0:T(8,128)S(1)}, f32[2,256,4,64]{1,3,2,0:T(8,128)}, u32[]{:S(2)}) copy-start(f32[2,256,4,64]{1,3,2,0:T(8,128)} %get-tuple-element.26) | copy-start | bytes 1572868
Sparse Core Ops, SparseCore 0:
  9.4 49.6 all-gather.2
  106.0 72.7 all-gather.4

commit v7 on v5

--- a/solution.py
+++ b/solution.py
@@ -137,12 +137,11 @@
     part1 = lax.all_to_all(jnp.broadcast_to(part1[None], (n_node,) + part1.shape), "node", 0, 0, tiled=True)
     sums1 = jnp.sum(part1, axis=0)
     gathered1 = lax.all_gather(inj1.reshape(subnets, rows, steps * cases), "node", axis=1, tiled=True)
-    prod1 = fast("srj,sjm->srm", impedance, gathered1).reshape(subnets, rows, steps, cases)
+    prod1 = fast("srj,sjm->smr", impedance, gathered1).reshape(subnets, steps, cases, rows)
     t1 = t0 + steps
     current1 = jnp.where(fault_step[:, None, :] <= t1[None, :, None], sums1 / denominator[:, None, :], 0.0)
-    volt1 = prod1 - current1[:, None] * fault_col[:, :, None, :]
-    volt = jnp.concatenate([volt0, volt1], axis=2)
-    return jnp.transpose(volt, (2, 0, 3, 1))
+    volt1 = prod1 - current1[..., None] * jnp.transpose(fault_col, (0, 2, 1))[:, None]
+    return jnp.concatenate([jnp.transpose(volt0, (2, 0, 3, 1)), jnp.transpose(volt1, (1, 0, 2, 3))], axis=0)
 
 
 def solution(mesh):

time: 199 us -> 200 us (level)
  matrix products: 53.2 us -> 56.6 us
  waiting for transfers between devices: 98.4 us -> 95.3 us
    dot_general x4, matrix products: 18.9 us -> 22.2 us  [mm(): jnp.einsum(spec, a, b, precision=PRECISE, preferred_element_type=jnp.floa...]
    all_gather x1, waiting for transfers between devices: 6.16 us -> 3.3 us  [body(): lax.all_gather(lax.optimization_barrier(source_amp), 'node', axis=2, tile...]
  transfers between devices with their start and end apart: 5 -> 5, of which waited for: 5 -> 5; matrix products, arithmetic and copies ran while one was open for 17% -> 19% of each run, Pallas kernels for 0% -> 0%
where the time goes in v7:
time: 200 us
  waiting for transfers between devices  95.3 us (48%)
  matrix products  56.6 us (28%)
  starting transfers between devices  19.8 us (10%)
  between operations  13.9 us (7%)
  local copies, waits for them, and re-layouts  7.47 us (4%)
  other arithmetic  6.6 us (3%)
    all_gather x1, waiting for transfers between devices, body(): lax.all_gather(inj1.reshape(subnets, rows, steps * cases), 'node', axis=1...  59.7 us
    dot_general x3, matrix products, fast(): jnp.einsum(spec, a, b, precision=lax.Precision.HIGH, preferred_element_ty...  27.8 us
    dot_general x4, matrix products, mm(): jnp.einsum(spec, a, b, precision=PRECISE, preferred_element_type=jnp.floa...  22.2 us
    all_to_all x1, waiting for transfers between devices, body(): incoming = lax.all_to_all(outgoing, ('region', 'node'), 0, 0, tiled=True)  18 us
    all_to_all x1, starting transfers between devices, body(): incoming = lax.all_to_all(outgoing, ('region', 'node'), 0, 0, tiled=True)  8.25 us
    all_to_all x1, starting transfers between devices, body(): small = lax.all_to_all(small, 'node', 0, 0, tiled=True)  7.99 us
    all_to_all x1, waiting for transfers between devices, body(): lax.all_to_all(jnp.broadcast_to(part1[None], (n_node,) + part1.shape), 'n...  7.38 us
    dot_general x4, matrix products, pick(): jnp.einsum(spec, a, b, precision=lax.Precision.HIGH, preferred_element_ty...  6.61 us
  transfers between devices with their start and end apart: 5, of which 5 were waited for; matrix products, arithmetic and copies ran while one was open for 19% of the time, Pallas kernels for 0%

profile of v7, /device:TPU:0, one launch (start us, length us, event | category | flops | bytes accessed | tf_op | source)
XLA Modules:
  0.0 199.6 jit_solution(3449649908752835358)
XLA Ops:
  6.5 0.7 all-gather.3.cloned.1.call-update
  7.3 0.7 copy.85
  8.0 13.1 %multiply_reduce_fusion.3 = (f32[1024]{0:T(1024)S(1)}, f32[1024]{0:T(1024)S(1)}, f32[1024]{0:T(1024)S(1)}, f32[1024]{0:T(1024)S(1)}, f32[1024]{0:T(1024)S(1)}, /...) fusion(f32[515,1024]{1,0:T(8,128)} %param.18, f32[512,1024]{1,0:T(8,128)} %param.17), kind=kOutput, calls=%fused_computation.15 | convolution fusion | flops 3230130176 | bytes 12648448 | tf_op jit(solution)/shard_map/uj,jk->uk/dot_general | solution.py:18
  21.1 0.8 fusion.12
  22.0 8.1 %multiply_reduce_fusion.10 = (f32[2,64]{1,0:T(2,128)S(1)}, f32[2,64]{1,0:T(2,128)S(1)}, f32[2,64]{1,0:T(2,128)S(1)}, f32[2,64,256]{2,1,0:T(8,128)S(1)}) fusion(f32[2,256]{1,0:T(2,128)S(1)} %get-tuple-element.40, f32[2,64,256]{2,1,0:T(8,128)S(1)} %copy-done, f32[2,256]{1,0:T(2,128)S(1)} %get-tuple-element.39, s32[2,64]{1,0:T(2,128)S(1)} %copy-done.8, ...), kind=kOutput, calls=%fused_computation.68 | convolution fusion | flops 1611431552 | bytes 8657920 | tf_op jit(solution)/shard_map/srj,sjc->src/dot_general | solution.py:18
  30.1 0.2 fusion.58
  30.6 0.7 broadcast_in_dim.23
  31.4 8.0 %all-to-all-start = ((f32[16,2,8,256]{3,2,1,0:T(8,128)}), f32[16,2,8,256]{3,2,1,0:T(8,128)S(1)}, u32[]{:S(2)}, u32[]{:S(2)}) async-start(f32[16,2,8,256]{3,2,1,0:T(8,128)} %broadcast_in_dim.23), calls=%async_computation | async-start | bytes 524288 | tf_op jit(solution)/shard_map/all_to_all | solution.py:88
  39.4 0.5 broadcast.180
  39.9 0.6 reduce.3
  40.5 0.1 eq.136
  40.7 0.7 fusion.7
  41.4 0.1 mul.361
  41.7 6.2 %all-to-all-done = f32[16,2,8,256]{3,2,1,0:T(8,128)S(1)} async-done(((f32[16,2,8,256]{3,2,1,0:T(8,128)}), f32[16,2,8,256]{3,2,1,0:T(8,128)S(1)}, u32[]{:S(2)}, u32[]{:S(2)}) %all-to-all-start) | async-done | bytes 262176 | tf_op jit(solution)/shard_map/all_to_all | solution.py:88
  48.1 0.1 broadcast_multiply_fusion.2
  48.2 0.4 copy.93
  48.7 6.9 %fusion.59 = f32[2,4,256]{2,1,0:T(4,128)S(1)} fusion(f32[2,4096,4]{1,2,0:T(4,128)S(1)} %bitcast.166, f32[2,256,4096]{2,1,0:T(8,128)} %param.14), kind=kOutput, calls=%fused_computation.98 | convolution fusion | flops 50331648 | bytes 8527872 | tf_op jit(solution)/shard_map/srj,sjt->srt/dot_general | solution.py:26
  55.6 0.1 add.156
  55.8 1.0 slice_cosine_fusion
  56.9 3.3 %all-gather.3.cloned.1.call-done = f32[2,64,4096]{2,1,0:T(8,128)} async-done(((f32[2,64,256]{2,1,0:T(8,128)}), f32[2,64,4096]{2,1,0:T(8,128)}) %all-gather.3.cloned.1.call-update) | async-done | bytes 2097168 | tf_op jit(solution)/shard_map/all_gather | solution.py:53
  60.2 2.1 %broadcast_multiply_fusion.1 = (f32[2,64,4096]{2,1,0:T(8,128)S(1)}, f32[2,64,4096]{2,1,0:T(8,128)S(1)}) fusion(f32[2,64,4096]{2,1,0:T(8,128)} %all-gather.3.cloned.1.call-done, f32[2,4096]{1,0:T(2,128)S(1)} %bitcast.169, f32[2,4096]{1,0:T(2,128)S(1)} %bitcast.170), kind=kLoop, calls=%fused_computation.44 | loop fusion | flops 1048576 | bytes 6356992 | tf_op jit(solution)/shard_map/mul | solution.py:93
  62.3 7.6 %fusion.28 = f32[2,256,128]{1,2,0:T(8,128)S(1)} fusion(f32[2,256,4096]{2,1,0:T(8,128)} %param.14, f32[2,64,4096]{2,1,0:T(8,128)S(1)} %get-tuple-element.17, f32[2,64,4096]{2,1,0:T(8,128)S(1)} %get-tuple-element.16), kind=kOutput, calls=%fused_computation.32 | convolution fusion | flops 1611661312 | bytes 12845056 | tf_op jit(solution)/shard_map/srj,scj->src/dot_general | solution.py:26
  70.0 0.1 copy.91
  70.1 0.1 mul.363
  70.3 0.1 copy.90
  70.4 0.1 mul.357
  70.6 0.2 add_subtract_fusion
  70.8 1.0 fusion.22
  71.8 2.3 %fusion.8 = f32[128,8,256]{2,1,0:T(8,128)} fusion(f32[1024,256,1]{0,1,2:T(8,128)S(1)} %bitcast.207, pred[128,8,1024]{2,0,1:T(32,128)(4,1)S(1)} %fusion.7), kind=kOutput, calls=%fused_computation.9 | convolution fusion | flops 1610612736 | bytes 3145728 | tf_op jit(solution)/shard_map/pk,km->pm/dot_general | solution.py:22
  74.1 8.2 %all-to-all-start.1 = ((f32[128,8,256]{2,1,0:T(8,128)}), f32[128,8,256]{2,1,0:T(8,128)S(1)}, u32[]{:S(2)}, u32[]{:S(2)}) async-start(f32[128,8,256]{2,1,0:T(8,128)} %fusion.8), calls=%async_computation.1 | async-start | bytes 2097152 | tf_op jit(solution)/shard_map/all_to_all | solution.py:120
  82.4 0.1 add_cosine_fusion
  82.6 0.8 slice_bitcast_fusion.1
  83.4 18.0 %all-to-all-done.1 = f32[128,8,256]{2,1,0:T(8,128)S(1)} async-done(((f32[128,8,256]{2,1,0:T(8,128)}), f32[128,8,256]{2,1,0:T(8,128)S(1)}, u32[]{:S(2)}, u32[]{:S(2)}) %all-to-all-start.1) | async-done | bytes 1048608 | tf_op jit(solution)/shard_map/all_to_all | solution.py:120
  101.4 0.3 copy.96
  101.7 1.6 fusion.5
  103.3 0.2 multiply_add_fusion
  103.5 1.7 multiply_reduce_fusion.8
  105.4 0.7 reshape.253
  106.1 3.5 %all-to-all-start.2 = ((f32[16,1,512]{2,1,0:T(1,128)}), f32[16,1,512]{2,1,0:T(1,128)S(1)}, u32[]{:S(2)}, u32[]{:S(2)}) async-start(f32[16,1,512]{2,1,0:T(1,128)} %reshape.253), calls=%async_computation.2 | async-start | bytes 65536 | tf_op jit(solution)/shard_map/all_to_all | solution.py:137
  109.6 0.2 multiply_subtract_fusion
  109.8 7.4 %all-to-all-done.2 = f32[16,1,512]{2,1,0:T(1,128)S(1)} async-done(((f32[16,1,512]{2,1,0:T(1,128)}), f32[16,1,512]{2,1,0:T(1,128)S(1)}, u32[]{:S(2)}, u32[]{:S(2)}) %all-to-all-start.2) | async-done | bytes 32800 | tf_op jit(solution)/shard_map/all_to_all | solution.py:137
  117.1 0.5 broadcast.181
  117.6 0.6 reduce.4
  118.3 0.1 reshape.254
  118.5 59.7 %all-gather.5.cloned.1.call-done = f32[2,4096,256]{1,2,0:T(8,128)} async-done(((f32[2,256,256]{1,2,0:T(8,128)}), f32[2,4096,256]{1,2,0:T(8,128)}) %all-gather.5.cloned.1.call-update) | async-done | bytes 8388624 | tf_op jit(solution)/shard_map/all_gather | solution.py:139
  178.2 13.3 %fusion.60 = f32[2,256,256]{2,1,0:T(8,128)S(1)} fusion(f32[2,4096,256]{1,2,0:T(8,128)} %all-gather.5.cloned.1.call-done, f32[2,256,4096]{2,1,0:T(8,128)} %param.14), kind=kOutput, calls=%fused_computation.99 | convolution fusion | flops 3221225472 | bytes 17301504 | tf_op jit(solution)/shard_map/srj,sjm->smr/dot_general | solution.py:26
  191.5 0.1 fusion.43
  191.7 1.1 pad_maximum_fusion
  (67 shorter events, 1.5 us)
Async XLA Ops:
  6.5 53.6 %all-gather.3.cloned.1.call-start = ((), (), s32[]{:S(2)}) async-start(), calls=%async_computation.3 | async-start | bytes 2228224 | tf_op jit(solution)/shard_map/all_gather | solution.py:53
  7.9 13.1 %copy-start.1 = (f32[2,256]{1,0:T(2,128)S(1)}, f32[2,256]{1,0:T(2,128)}, u32[]{:S(2)}) copy-start(f32[2,256]{1,0:T(2,128)} %param.16) | copy-start | bytes 6148
  7.9 13.2 %copy-start.10 = (s32[1024]{0:T(1024)S(1)}, s32[1024]{0:T(1024)}, u32[]{:S(2)}) copy-start(s32[1024]{0:T(1024)} %param.20) | copy-start | bytes 12292
  8.0 14.0 %copy-start = (f32[2,64,256]{2,1,0:T(8,128)S(1)}, f32[2,64,256]{2,1,0:T(8,128)}, u32[]{:S(2)}) copy-start(f32[2,64,256]{2,1,0:T(8,128)} %param.15) | copy-start | bytes 393220
  8.0 14.0 %copy-start.8 = (s32[2,64]{1,0:T(2,128)S(1)}, s32[2,64]{1,0:T(2,128)}, u32[]{:S(2)}) copy-start(s32[2,64]{1,0:T(2,128)} %param.22) | copy-start | bytes 1540
  21.9 17.9 %copy-start.6 = (s32[1,1024]{1,0:T(1,128)S(1)}, s32[1,1024]{1,0:T(1,128)}, u32[]{:S(2)}) copy-start(s32[1,1024]{1,0:T(1,128)} %param.21) | copy-start | bytes 12292
  30.1 11.3 %copy-start.3 = (f32[4]{0:T(128)S(1)}, f32[4]{0:T(128)}, u32[]{:S(2)}) copy-start(f32[4]{0:T(128)} %constant.26.clone) | copy-start | bytes 52
  30.1 11.5 %copy-start.4 = (f32[4]{0:T(128)S(1)}, f32[4]{0:T(128)}, u32[]{:S(2)}) copy-start(f32[4]{0:T(128)} %constant.8.clone) | copy-start | bytes 52
  30.1 11.6 %copy-start.5 = (f32[1024]{0:T(1024)S(1)}, f32[1024]{0:T(1024)}, u32[]{:S(2)}) copy-start(f32[1024]{0:T(1024)} %param.19) | copy-start | bytes 12292
  30.1 17.9 %copy-start.7 = (f32[2,64]{1,0:T(2,128)S(1)}, f32[2,64]{1,0:T(2,128)}, u32[]{:S(2)}) copy-start(f32[2,64]{1,0:T(2,128)} %param.24) | copy-start | bytes 1540
  30.1 17.9 %copy-start.2 = (s32[2,64]{1,0:T(2,128)S(1)}, s32[2,64]{1,0:T(2,128)}, u32[]{:S(2)}) copy-start(s32[2,64]{1,0:T(2,128)} %param.23) | copy-start | bytes 1540
  31.4 16.5 %all-to-all-start = ((f32[16,2,8,256]{3,2,1,0:T(8,128)}), f32[16,2,8,256]{3,2,1,0:T(8,128)S(1)}, u32[]{:S(2)}, u32[]{:S(2)}) async-start(f32[16,2,8,256]{3,2,1,0:T(8,128)} %broadcast_in_dim.23), calls=%async_computation | async-start | bytes 524288 | tf_op jit(solution)/shard_map/all_to_all | solution.py:88
  74.1 8.3 %copy-start.9 = (f32[4]{0:T(128)S(1)}, f32[4]{0:T(128)}, u32[]{:S(2)}) copy-start(f32[4]{0:T(128)} %constant.27.clone) | copy-start | bytes 52
  74.1 27.3 %all-to-all-start.1 = ((f32[128,8,256]{2,1,0:T(8,128)}), f32[128,8,256]{2,1,0:T(8,128)S(1)}, u32[]{:S(2)}, u32[]{:S(2)}) async-start(f32[128,8,256]{2,1,0:T(8,128)} %fusion.8), calls=%async_computation.1 | async-start | bytes 2097152 | tf_op jit(solution)/shard_map/all_to_all | solution.py:120
  82.3 95.9 %all-gather.5.cloned.1.call-start = ((), (), s32[]{:S(2)}) async-start(), calls=%async_computation.4 | async-start | bytes 8912896 | tf_op jit(solution)/shard_map/all_gather | solution.py:139
  106.1 11.0 %all-to-all-start.2 = ((f32[16,1,512]{2,1,0:T(1,128)}), f32[16,1,512]{2,1,0:T(1,128)S(1)}, u32[]{:S(2)}, u32[]{:S(2)}) async-start(f32[16,1,512]{2,1,0:T(1,128)} %reshape.253), calls=%async_computation.2 | async-start | bytes 65536 | tf_op jit(solution)/shard_map/all_to_all | solution.py:137
Sparse Core Ops, SparseCore 0:
  9.4 50.6 all-gather.2
  105.4 72.7 all-gather.4

commit v8 on v5

--- a/solution.py
+++ b/solution.py
@@ -59,7 +59,7 @@
     attach_mapT = (local_ids[:, None] == attach[None, :]).astype(jnp.float32)
 
     onehotT = (lax.iota(jnp.int32, order)[None, :, None] == fault_node[:, None, :]).astype(jnp.float32)
-    fault_col = mm("srj,sjc->src", impedance, onehotT)
+    fault_col = pick("srj,sjc->src", impedance, onehotT)
     owner = (row_ids[None, :, None] == fault_node[:, None, :]).astype(jnp.float32)
     self_part = jnp.sum(fault_col * owner, axis=1)
 

time: 199 us -> 199 us (level)
    dot_general x4 -> x3, matrix products: 18.9 us -> 14.2 us  [mm(): jnp.einsum(spec, a, b, precision=PRECISE, preferred_element_type=jnp.floa...]
    dot_general x4 -> x5, matrix products: 6.62 us -> 9.44 us  [pick(): jnp.einsum(spec, a, b, precision=lax.Precision.HIGH, preferred_element_ty...]
  transfers between devices with their start and end apart: 5 -> 5, of which waited for: 5 -> 5; matrix products, arithmetic and copies ran while one was open for 17% -> 16% of each run, Pallas kernels for 0% -> 0%
where the time goes in v8:
time: 199 us
  waiting for transfers between devices  100 us (50%)
  matrix products  51.3 us (26%)
  starting transfers between devices  19.4 us (10%)
  between operations  13.9 us (7%)
  local copies, waits for them, and re-layouts  8.51 us (4%)
  other arithmetic  5.41 us (3%)
    all_gather x1, waiting for transfers between devices, body(): lax.all_gather(inj1.reshape(subnets, rows, steps * cases), 'node', axis=1...  59.8 us
    dot_general x3, matrix products, fast(): jnp.einsum(spec, a, b, precision=lax.Precision.HIGH, preferred_element_ty...  27.7 us
    all_to_all x1, waiting for transfers between devices, body(): incoming = lax.all_to_all(outgoing, ('region', 'node'), 0, 0, tiled=True)  18 us
    dot_general x3, matrix products, mm(): jnp.einsum(spec, a, b, precision=PRECISE, preferred_element_type=jnp.floa...  14.2 us
    dot_general x5, matrix products, pick(): jnp.einsum(spec, a, b, precision=lax.Precision.HIGH, preferred_element_ty...  9.44 us
    all_gather x1, waiting for transfers between devices, body(): lax.all_gather(lax.optimization_barrier(source_amp), 'node', axis=2, tile...  8.09 us
    all_to_all x1, starting transfers between devices, body(): small = lax.all_to_all(small, 'node', 0, 0, tiled=True)  8 us
    all_to_all x1, starting transfers between devices, body(): incoming = lax.all_to_all(outgoing, ('region', 'node'), 0, 0, tiled=True)  7.91 us
  transfers between devices with their start and end apart: 5, of which 5 were waited for; matrix products, arithmetic and copies ran while one was open for 16% of the time, Pallas kernels for 0%

profile of v8, /device:TPU:0, one launch (start us, length us, event | category | flops | bytes accessed | tf_op | source)
XLA Modules:
  0.0 198.9 jit_solution(12183468843780407230)
XLA Ops:
  6.5 0.7 all-gather.3.cloned.1.call-update
  7.3 0.7 fusion.57
  8.1 13.1 %multiply_reduce_fusion.3 = (f32[1024]{0:T(1024)S(1)}, f32[1024]{0:T(1024)S(1)}, f32[1024]{0:T(1024)S(1)}, f32[1024]{0:T(1024)S(1)}, f32[1024]{0:T(1024)S(1)}, /...) fusion(f32[515,1024]{1,0:T(8,128)} %param.18, f32[512,1024]{1,0:T(8,128)} %param.17), kind=kOutput, calls=%fused_computation.15 | convolution fusion | flops 3230130176 | bytes 12648448 | tf_op jit(solution)/shard_map/uj,jk->uk/dot_general | solution.py:18
  21.2 0.8 fusion.12
  22.1 2.8 %multiply_reduce_fusion.10 = (f32[2,64]{1,0:T(2,128)S(1)}, f32[2,64]{1,0:T(2,128)S(1)}, f32[2,64]{1,0:T(2,128)S(1)}, f32[2,64,256]{2,1,0:T(8,128)S(1)}) fusion(f32[2,256]{1,0:T(2,128)S(1)} %get-tuple-element.40, f32[2,64,256]{2,1,0:T(8,128)S(1)} %copy-done, f32[2,256]{1,0:T(2,128)S(1)} %get-tuple-element.39, s32[2,64]{1,0:T(2,128)S(1)} %copy-done.8, ...), kind=kOutput, calls=%fused_computation.68 | convolution fusion | flops 806125184 | bytes 8657920 | tf_op jit(solution)/shard_map/srj,sjc->src/dot_general | solution.py:22
  25.0 0.2 fusion.58
  25.5 0.7 broadcast_in_dim.23
  26.2 8.0 %all-to-all-start = ((f32[16,2,8,256]{3,2,1,0:T(8,128)}), f32[16,2,8,256]{3,2,1,0:T(8,128)S(1)}, u32[]{:S(2)}, u32[]{:S(2)}) async-start(f32[16,2,8,256]{3,2,1,0:T(8,128)} %broadcast_in_dim.23), calls=%async_computation | async-start | bytes 524288 | tf_op jit(solution)/shard_map/all_to_all | solution.py:88
  34.2 0.5 broadcast.177
  34.8 0.6 reduce.3
  35.4 0.1 eq.136
  35.5 0.7 fusion.7
  36.3 0.1 mul.331
  36.6 6.2 %all-to-all-done = f32[16,2,8,256]{3,2,1,0:T(8,128)S(1)} async-done(((f32[16,2,8,256]{3,2,1,0:T(8,128)}), f32[16,2,8,256]{3,2,1,0:T(8,128)S(1)}, u32[]{:S(2)}, u32[]{:S(2)}) %all-to-all-start) | async-done | bytes 262176 | tf_op jit(solution)/shard_map/all_to_all | solution.py:88
  42.7 1.0 slice_cosine_fusion
  44.0 6.7 %convolution_bitcast_fusion = f32[2,256,4]{1,2,0:T(4,128)S(1)} fusion(f32[2,4096,4]{1,2,0:T(4,128)S(1)} %bitcast.165, f32[2,256,4096]{2,1,0:T(8,128)} %param.14), kind=kOutput, calls=%fused_computation.33 | convolution fusion | flops 50331648 | bytes 8527872 | tf_op jit(solution)/shard_map/srj,sjt->srt/dot_general | solution.py:26
  50.7 0.1 add.142.clone
  51.0 8.1 %all-gather.3.cloned.1.call-done = f32[2,64,4096]{2,1,0:T(8,128)} async-done(((f32[2,64,256]{2,1,0:T(8,128)}), f32[2,64,4096]{2,1,0:T(8,128)}) %all-gather.3.cloned.1.call-update) | async-done | bytes 2097168 | tf_op jit(solution)/shard_map/all_gather | solution.py:53
  59.1 2.1 %broadcast_multiply_fusion.1 = (f32[2,64,4096]{2,1,0:T(8,128)S(1)}, f32[2,64,4096]{2,1,0:T(8,128)S(1)}) fusion(f32[2,64,4096]{2,1,0:T(8,128)} %all-gather.3.cloned.1.call-done, f32[2,4096]{1,0:T(2,128)S(1)} %bitcast.168, f32[2,4096]{1,0:T(2,128)S(1)} %bitcast.169), kind=kLoop, calls=%fused_computation.45 | loop fusion | flops 1048576 | bytes 6356992 | tf_op jit(solution)/shard_map/mul | solution.py:93
  61.3 7.6 %fusion.28 = f32[2,256,128]{1,2,0:T(8,128)S(1)} fusion(f32[2,256,4096]{2,1,0:T(8,128)} %param.14, f32[2,64,4096]{2,1,0:T(8,128)S(1)} %get-tuple-element.17, f32[2,64,4096]{2,1,0:T(8,128)S(1)} %get-tuple-element.16), kind=kOutput, calls=%fused_computation.32 | convolution fusion | flops 1611661312 | bytes 12845056 | tf_op jit(solution)/shard_map/srj,scj->src/dot_general | solution.py:26
  69.0 0.1 copy.93
  69.1 0.1 copy.94
  69.2 0.2 add_subtract_fusion.1
  69.4 0.4 copy.79
  69.8 0.1 mul.303.clone
  70.0 0.1 mul.306.clone
  70.2 0.2 add_subtract_fusion
  70.4 1.0 fusion.22
  71.4 2.3 %fusion.8 = f32[128,8,256]{2,1,0:T(8,128)} fusion(f32[1024,256,1]{0,1,2:T(8,128)S(1)} %bitcast.202, pred[128,8,1024]{2,0,1:T(32,128)(4,1)S(1)} %fusion.7), kind=kOutput, calls=%fused_computation.9 | convolution fusion | flops 1610612736 | bytes 3145728 | tf_op jit(solution)/shard_map/pk,km->pm/dot_general | solution.py:22
  73.7 7.9 %all-to-all-start.1 = ((f32[128,8,256]{2,1,0:T(8,128)}), f32[128,8,256]{2,1,0:T(8,128)S(1)}, u32[]{:S(2)}, u32[]{:S(2)}) async-start(f32[128,8,256]{2,1,0:T(8,128)} %fusion.8), calls=%async_computation.1 | async-start | bytes 2097152 | tf_op jit(solution)/shard_map/all_to_all | solution.py:120
  81.7 0.1 add_cosine_fusion
  81.9 0.8 slice_bitcast_fusion.1
  82.6 18.0 %all-to-all-done.1 = f32[128,8,256]{2,1,0:T(8,128)S(1)} async-done(((f32[128,8,256]{2,1,0:T(8,128)}), f32[128,8,256]{2,1,0:T(8,128)S(1)}, u32[]{:S(2)}, u32[]{:S(2)}) %all-to-all-start.1) | async-done | bytes 1048608 | tf_op jit(solution)/shard_map/all_to_all | solution.py:120
  100.6 0.3 copy.82
  101.0 1.6 fusion.5
  102.6 0.2 multiply_add_fusion
  102.8 1.7 multiply_reduce_fusion.8
  104.5 0.7 reshape.252
  105.2 3.5 %all-to-all-start.2 = ((f32[16,1,512]{2,1,0:T(1,128)}), f32[16,1,512]{2,1,0:T(1,128)S(1)}, u32[]{:S(2)}, u32[]{:S(2)}) async-start(f32[16,1,512]{2,1,0:T(1,128)} %reshape.252), calls=%async_computation.2 | async-start | bytes 65536 | tf_op jit(solution)/shard_map/all_to_all | solution.py:137
  108.7 7.6 %all-to-all-done.2 = f32[16,1,512]{2,1,0:T(1,128)S(1)} async-done(((f32[16,1,512]{2,1,0:T(1,128)}), f32[16,1,512]{2,1,0:T(1,128)S(1)}, u32[]{:S(2)}, u32[]{:S(2)}) %all-to-all-start.2) | async-done | bytes 32800 | tf_op jit(solution)/shard_map/all_to_all | solution.py:137
  116.3 0.5 broadcast.178
  116.8 0.6 reduce.4
  117.4 0.1 reshape.253
  117.6 59.8 %all-gather.5.cloned.1.call-done = f32[2,4096,256]{1,2,0:T(8,128)} async-done(((f32[2,256,256]{1,2,0:T(8,128)}), f32[2,4096,256]{1,2,0:T(8,128)}) %all-gather.5.cloned.1.call-update) | async-done | bytes 8388624 | tf_op jit(solution)/shard_map/all_gather | solution.py:139
  177.5 13.3 %fusion.59 = f32[2,256,256]{2,1,0:T(8,128)S(1)} fusion(f32[2,4096,256]{1,2,0:T(8,128)} %all-gather.5.cloned.1.call-done, f32[2,256,4096]{2,1,0:T(8,128)} %param.14), kind=kOutput, calls=%fused_computation.97 | convolution fusion | flops 3221225472 | bytes 17301504 | tf_op jit(solution)/shard_map/srj,sjm->srm/dot_general | solution.py:26
  190.8 0.1 multiply_subtract_fusion
  190.9 0.1 maximum_bitcast_fusion.2
  191.0 1.1 copy.84
  (68 shorter events, 1.4 us)
Async XLA Ops:
  6.5 52.6 %all-gather.3.cloned.1.call-start = ((), (), s32[]{:S(2)}) async-start(), calls=%async_computation.3 | async-start | bytes 2228224 | tf_op jit(solution)/shard_map/all_gather | solution.py:53
  8.0 14.1 %slice-start = ((s8[8388608]{0:T(1024)(128)(4,1)}), s8[4194304]{0:T(1024)(128)(4,1)S(1)}, s32[]{:S(2)}) async-start(s8[8388608]{0:T(1024)(128)(4,1)} %bitcast.148), calls=%async_computation.5 | async-start | bytes 8388608
  8.0 13.2 %copy-start.10 = (s32[1024]{0:T(1024)S(1)}, s32[1024]{0:T(1024)}, u32[]{:S(2)}) copy-start(s32[1024]{0:T(1024)} %param.20) | copy-start | bytes 12292
  8.0 14.0 %slice-start.1 = ((s8[8388608]{0:T(1024)(128)(4,1)}), s8[4194304]{0:T(1024)(128)(4,1)S(1)}, s32[]{:S(2)}) async-start(s8[8388608]{0:T(1024)(128)(4,1)} %bitcast.148), calls=%async_computation.6 | async-start | bytes 8388608
  8.0 14.0 %copy-start = (f32[2,64,256]{2,1,0:T(8,128)S(1)}, f32[2,64,256]{2,1,0:T(8,128)}, u32[]{:S(2)}) copy-start(f32[2,64,256]{2,1,0:T(8,128)} %param.15) | copy-start | bytes 393220
  8.1 14.0 %copy-start.8 = (s32[2,64]{1,0:T(2,128)S(1)}, s32[2,64]{1,0:T(2,128)}, u32[]{:S(2)}) copy-start(s32[2,64]{1,0:T(2,128)} %param.22) | copy-start | bytes 1540
  22.1 3.2 %copy-start.1 = (f32[2,256]{1,0:T(2,128)S(1)}, f32[2,256]{1,0:T(2,128)}, u32[]{:S(2)}) copy-start(f32[2,256]{1,0:T(2,128)} %param.16) | copy-start | bytes 6148
  22.1 12.6 %copy-start.5 = (s32[1,1024]{1,0:T(1,128)S(1)}, s32[1,1024]{1,0:T(1,128)}, u32[]{:S(2)}) copy-start(s32[1,1024]{1,0:T(1,128)} %param.21) | copy-start | bytes 12292
  24.9 11.3 %copy-start.2 = (f32[4]{0:T(128)S(1)}, f32[4]{0:T(128)}, u32[]{:S(2)}) copy-start(f32[4]{0:T(128)} %constant.8.clone) | copy-start | bytes 52
  25.0 11.4 %copy-start.3 = (f32[4]{0:T(128)S(1)}, f32[4]{0:T(128)}, u32[]{:S(2)}) copy-start(f32[4]{0:T(128)} %constant.26.clone) | copy-start | bytes 52
  25.0 11.6 %copy-start.4 = (f32[1024]{0:T(1024)S(1)}, f32[1024]{0:T(1024)}, u32[]{:S(2)}) copy-start(f32[1024]{0:T(1024)} %param.19) | copy-start | bytes 12292
  26.2 16.5 %all-to-all-start = ((f32[16,2,8,256]{3,2,1,0:T(8,128)}), f32[16,2,8,256]{3,2,1,0:T(8,128)S(1)}, u32[]{:S(2)}, u32[]{:S(2)}) async-start(f32[16,2,8,256]{3,2,1,0:T(8,128)} %broadcast_in_dim.23), calls=%async_computation | async-start | bytes 524288 | tf_op jit(solution)/shard_map/all_to_all | solution.py:88
  43.9 7.0 %copy-start.7 = (f32[2,64]{1,0:T(2,128)S(1)}, f32[2,64]{1,0:T(2,128)}, u32[]{:S(2)}) copy-start(f32[2,64]{1,0:T(2,128)} %param.24) | copy-start | bytes 1540
  44.0 7.0 %copy-start.6 = (s32[2,64]{1,0:T(2,128)S(1)}, s32[2,64]{1,0:T(2,128)}, u32[]{:S(2)}) copy-start(s32[2,64]{1,0:T(2,128)} %param.23) | copy-start | bytes 1540
  73.7 8.0 %copy-start.9 = (f32[4]{0:T(128)S(1)}, f32[4]{0:T(128)}, u32[]{:S(2)}) copy-start(f32[4]{0:T(128)} %constant.27.clone) | copy-start | bytes 52
  73.7 26.9 %all-to-all-start.1 = ((f32[128,8,256]{2,1,0:T(8,128)}), f32[128,8,256]{2,1,0:T(8,128)S(1)}, u32[]{:S(2)}, u32[]{:S(2)}) async-start(f32[128,8,256]{2,1,0:T(8,128)} %fusion.8), calls=%async_computation.1 | async-start | bytes 2097152 | tf_op jit(solution)/shard_map/all_to_all | solution.py:120
  81.6 95.9 %all-gather.5.cloned.1.call-start = ((), (), s32[]{:S(2)}) async-start(), calls=%async_computation.4 | async-start | bytes 8912896 | tf_op jit(solution)/shard_map/all_gather | solution.py:139
  105.2 11.0 %all-to-all-start.2 = ((f32[16,1,512]{2,1,0:T(1,128)}), f32[16,1,512]{2,1,0:T(1,128)S(1)}, u32[]{:S(2)}, u32[]{:S(2)}) async-start(f32[16,1,512]{2,1,0:T(1,128)} %reshape.252), calls=%async_computation.2 | async-start | bytes 65536 | tf_op jit(solution)/shard_map/all_to_all | solution.py:137
Sparse Core Ops, SparseCore 0:
  9.4 49.6 all-gather.2
  104.6 72.7 all-gather.4
